TPU v7x, 256 devices: a whole 4x4x8 slice. The times are simulated.
256 devices in a mesh: dp: 32 (over z, y_hi, core), inner: 8 (over y_lo, x).
Axes of the slice: x: 4, y: 4 (y_hi: 2, y_lo: 2; y = y_hi * 2 + y_lo), z: 8, core: 2. Of those that a mesh axis runs over, the one named last changes fastest.
Arguments:
- tokens: bfloat16 [131072, 1664], P(('dp', 'inner')), may hold values from -16 to 16
- attn_gain: float32 [1664], replicated, may hold values from 0.1 to 1.9
- qkv_weight: bfloat16 [3, 1664, 832], P(None, 'dp', 'inner'), may hold values from -6 to 6
- out_weight: bfloat16 [832, 1664], P('inner', 'dp'), may hold values from -0.21875 to 0.21875
- merge_gain: float32 [6656], replicated, may hold values from 0.25 to 1.75
- merge_weight: bfloat16 [6656, 2048], P('dp', 'inner'), may hold values from -0.078125 to 0.078125
- segment_ids: int32 [131072], P('dp'), may hold values from -1 to 7, as said below
- owners: int32 [32768, 1], P('dp'), may hold values from 0 to 31; in each aligned block of 1024 rows (0 to 1023, 1024 to 2047, ...) at most 64 rows name the same one
Outputs:
- merged_out: bfloat16 [65536, 2048], P('dp', 'inner')
Inputs may be any that keep to these rules, and one draw needn't show every extreme that they name: `segment_ids`: within each device's aligned block of 512 tokens, ids never fall except to -1, which fills a tail of 4 or more tokens; every run of one id starts at a multiple of 4 and holds a multiple of 4 tokens. `owners`: in each aligned block of 1024 rows (the rows of one index of dp) no owner is named by more than 64 rows.
All inputs are finite; a program needn't handle non-finite values.
Results may differ from a plain program's by a relative error of at most 0.0062.
Values may be sent and summed in bfloat16 or wider, within the bound.
No kernel may reach another device: no remote copies, remote signals or barrier semaphores. Data moves between devices by JAX's collectives and lax.ppermute only.
A program may use at most 128 MiB of HBM per device.

v0:
```python
import jax
import jax.numpy as jnp
from jax import lax
from jax.sharding import PartitionSpec as P

HEAD_DIM = 104


EPS = 1e-06
NEG = -1e30


def layer_norm(values, gain):
    values = values.astype(jnp.float32)
    center = values - jnp.mean(values, axis=-1, keepdims=True)
    spread = jnp.mean(center * center, axis=-1, keepdims=True)
    return center * lax.rsqrt(spread + EPS) * gain


def attend_block(queries, keys, vectors, segment):
    scale = queries.shape[-1] ** (-0.5)
    scores = jnp.einsum("qhe,khe->hqk", queries, keys, preferred_element_type=jnp.float32) * scale
    visible = segment[:, None] == segment[None, :]
    scores = jnp.where(visible[None, :, :], scores, NEG)
    top = jnp.max(scores, axis=-1, keepdims=True)
    weights = jnp.exp(scores - top)
    probs = (weights / jnp.sum(weights, axis=-1, keepdims=True)).astype(jnp.bfloat16)
    context = jnp.einsum("hqk,khe->qhe", probs, vectors, preferred_element_type=jnp.float32)
    return context.astype(jnp.bfloat16)


def split_heads(projected):
    shaped = projected.reshape(3, projected.shape[1], projected.shape[2] // HEAD_DIM, HEAD_DIM)
    return (shaped[0], shaped[1], shaped[2])


def local(tokens, attn_gain, qkv_weight, out_weight, merge_gain, merge_weight, segment_ids, owners):
    tok_rows = tokens.shape[0]
    local_segment = lax.dynamic_slice_in_dim(
        segment_ids, lax.axis_index("inner") * tok_rows, tok_rows
    )
    normed = layer_norm(tokens, attn_gain).astype(jnp.bfloat16)
    qkv_part = lax.all_gather(qkv_weight, "inner", axis=2, tiled=True)
    projected = jnp.einsum(
        "td,cdh->cth",
        normed,
        lax.all_gather(qkv_part, "dp", axis=1, tiled=True),
        preferred_element_type=jnp.float32,
    )
    queries, keys, vectors = split_heads(projected.astype(jnp.bfloat16))
    context = attend_block(queries, keys, vectors, local_segment).reshape(tok_rows, -1)
    out_part = lax.all_gather(out_weight, "inner", axis=0, tiled=True)
    attn_out = jnp.dot(
        context,
        lax.all_gather(out_part, "dp", axis=1, tiled=True),
        preferred_element_type=jnp.float32,
    )
    hidden = tokens.astype(jnp.float32) + attn_out
    quad_rows = hidden.reshape(tok_rows // 4, -1)
    live = local_segment.reshape(-1, 4)[:, 0] >= 0
    merged = jnp.where(live[:, None], layer_norm(quad_rows, merge_gain), 0.0).astype(jnp.bfloat16)
    merge_full = lax.all_gather(merge_weight, "dp", axis=0, tiled=True)
    features = jnp.dot(
        lax.all_gather(merged, "inner", axis=0, tiled=True),
        merge_full,
        preferred_element_type=jnp.float32,
    ).astype(jnp.bfloat16)
    n_dp = lax.axis_size("dp")
    group_rows = features.shape[0]
    slots = 2 * group_rows // n_dp
    owner_col = owners[:, 0]
    chosen = (owner_col[:, None] == jnp.arange(n_dp, dtype=jnp.int32)[None, :]).astype(jnp.int32)
    earlier = jnp.cumsum(chosen, axis=0) - chosen
    rank = jnp.sum(earlier * chosen, axis=1)
    target = owner_col * slots + rank
    source_row = (
        jnp.full((n_dp * slots,), group_rows, jnp.int32)
        .at[target]
        .set(jnp.arange(group_rows, dtype=jnp.int32))
    )
    padded = jnp.concatenate([features, jnp.zeros((1, features.shape[1]), jnp.bfloat16)], axis=0)
    outgoing = padded[source_row]
    return lax.all_to_all(outgoing, "dp", split_axis=0, concat_axis=0, tiled=True)


def solution(mesh):
    placed = (
        P(("dp", "inner"), None),
        P(),
        P(None, "dp", "inner"),
        P("inner", "dp"),
        P(),
        P("dp", "inner"),
        P("dp"),
        P("dp", None),
    )
    return jax.shard_map(
        local, mesh=mesh, in_specs=placed, out_specs=P("dp", "inner"), check_vma=False
    )
```

profile of v0, /device:TPU:30, one launch (start us, length us, event | category | flops | bytes accessed | tf_op | source)
XLA Modules:
  0.0 521.2 jit_solution(5814935744648838367)
XLA Ops:
  6.5 28.6 %all-gather = bf16[8,104,52]{1,2,0:T(8,128)(2,1)S(1)} all-gather(bf16[1,104,52]{1,2,0:T(8,128)(2,1)} %bitcast.61), channel_id=1, replica_groups=mesh['dp'=32,'inner'=8] {'inner'}, dimensions={0}, use_global_device_ids=true | all-gather | bytes 97344 | tf_op jit(solution)/shard_map/all_gather | solution.py:52
  35.1 0.8 reshape.115
  36.0 0.9 copy.18
  36.9 29.9 %all_gather.18 = bf16[3,52,832]{1,0,2:T(4,128)(2,1)S(1)} all-gather(bf16[3,52,104]{1,0,2:T(4,128)(2,1)S(1)} %copy.18), channel_id=1, replica_groups=mesh['dp'=32,'inner'=8] {'inner'}, dimensions={2}, use_global_device_ids=true | all-gather | bytes 292032 | tf_op jit(solution)/shard_map/all_gather | solution.py:43
  66.7 1.7 copy.19
  68.5 0.7 all-gather.11.cloned.1.call-update
  69.3 0.3 convert_reduce_fusion
  69.6 0.6 fusion.10
  70.2 0.8 dynamic_slice.3
  71.2 0.9 broadcast_compare_fusion
  72.1 47.9 %all-gather.13.cloned.1.call-done = bf16[32,52,832]{2,1,0:T(8,128)(2,1)} async-done(((bf16[1,52,832]{2,1,0:T(8,128)(2,1)}), bf16[32,52,832]{2,1,0:T(8,128)(2,1)}) %all-gather.13.cloned.1.call-update) | async-done | bytes 2768912 | tf_op jit(solution)/shard_map/all_gather | solution.py:55
  120.0 5.6 %reshape.117 = bf16[1664,832]{1,0:T(8,128)(2,1)} reshape(bf16[32,52,832]{2,1,0:T(8,128)(2,1)} %all-gather.13.cloned.1.call-done) | data formatting | bytes 5537792
  125.7 108.2 %all-gather.7.cloned.1.call-done = bf16[3,1664,832]{2,0,1:T(4,128)(2,1)} async-done(((bf16[3,52,832]{2,0,1:T(4,128)(2,1)}), bf16[3,1664,832]{2,0,1:T(4,128)(2,1)}) %all-gather.7.cloned.1.call-update) | async-done | bytes 8306704 | tf_op jit(solution)/shard_map/all_gather | solution.py:47
  233.8 12.2 %convert_bitcast_fusion = bf16[3,512,832]{1,2,0:T(8,128)(2,1)S(1)} fusion(bf16[3,1664,832]{2,0,1:T(4,128)(2,1)} %all-gather.7.cloned.1.call-done, bf16[512,1664]{1,0:T(8,128)(2,1)S(1)} %copy-done, f32[1664]{0:T(1024)S(1)} %copy-done.4, f32[512]{0:T(512)S(1)} %add_rsqrt_fusion, f32[512]{0:T(512)S(1)} %broadcast_multiply_fusion), kind=kOutput, calls=%fused_computation.23 | convolution fusion | flops 4258562048 | bytes 12577280 | tf_op jit(solution)/shard_map/td,cdh->cth/dot_general | solution.py:44
  246.0 1.1 fusion.33
  247.1 7.8 %fusion.34 = (f32[8,512]{1,0:T(8,128)S(1)}, f32[8,512,512]{1,2,0:T(8,128)}) fusion(pred[512,512]{0,1:T(8,128)(4,1)} %broadcast_compare_fusion, bf16[512,8,104]{0,2,1:T(8,128)(2,1)} %bitcast.54, bf16[512,8,104]{0,2,1:T(8,128)(2,1)S(1)} %bitcast.53), kind=kOutput, calls=%fused_computation.54 | convolution fusion | flops 444596736 | bytes 10371072 | tf_op jit(solution)/shard_map/sub | solution.py:26
  254.9 4.3 fusion.20
  259.2 3.9 fusion.35
  263.4 0.1 sub.43
  263.6 2.9 reshape.95
  266.5 2.5 multiply_reduce_fusion
  269.0 0.1 reduce_sum.77
  269.2 1.8 select_convert_fusion
  271.1 9.2 %reduce-window.6 = s32[32,8,128]{2,1,0:T(8,128)S(1)} reduce-window(s32[32,8,128]{2,1,0:T(8,128)S(1)} %fusion.26, s32[]{:T(128)} %constant.18.clone.1), window={size=1x1x128 pad=0_0x0_0x127_0}, to_apply=%region_8.9 | reduce-window | flops 4161536 | bytes 262148 | tf_op jit(solution)/shard_map/reduce-window
  280.4 0.1 copy.23
  280.8 4.3 scatter_custom_fusion
  285.2 32.0 %all-gather.11.cloned.1.call-done = bf16[6656,256]{1,0:T(8,128)(2,1)} async-done(((bf16[208,256]{1,0:T(8,128)(2,1)}), bf16[6656,256]{1,0:T(8,128)(2,1)}) %all-gather.11.cloned.1.call-update) | async-done | bytes 3407888 | tf_op jit(solution)/shard_map/all_gather | solution.py:62
  317.2 140.6 %all-gather.9.cloned.1.call-done = bf16[1024,6656]{1,0:T(8,128)(2,1)} async-done(((bf16[128,6656]{1,0:T(8,128)(2,1)}), bf16[1024,6656]{1,0:T(8,128)(2,1)}) %all-gather.9.cloned.1.call-update) | async-done | bytes 13631504 | tf_op jit(solution)/shard_map/all_gather | solution.py:64
  457.8 9.5 %convolution_convert_fusion = bf16[1024,256]{1,0:T(8,128)(2,1)S(1)} fusion(bf16[1024,6656]{1,0:T(8,128)(2,1)} %all-gather.9.cloned.1.call-done, bf16[6656,256]{1,0:T(8,128)(2,1)} %all-gather.11.cloned.1.call-done), kind=kOutput, calls=%fused_computation.29 | convolution fusion | flops 3489923072 | bytes 17563648 | tf_op jit(solution)/shard_map/dot_general | solution.py:63
  467.3 7.5 %gather_fusion = bf16[2048,256]{1,0:T(8,128)(2,1)S(1)} fusion(bf16[1025,256]{1,0:T(8,128)(2,1)S(1)} %concatenate.3, s32[2048]{0:T(1024)S(1)} %fusion.28), kind=kCustom, calls=%fused_computation | custom fusion | bytes 2105344 | tf_op jit(solution)/shard_map/gather | solution.py:82
  474.8 38.8 %all_to_all.12 = bf16[32,64,256]{2,1,0:T(8,128)(2,1)S(1)} all-to-all(bf16[32,64,256]{2,1,0:T(8,128)(2,1)S(1)} %bitcast.51), channel_id=1, replica_groups=mesh['dp'=32,'inner'=8] {'dp'}, dimensions={0} | all-to-all | bytes 2097152 | tf_op jit(solution)/shard_map/all_to_all | solution.py:83
  513.7 1.0 copy.33
  (39 shorter events, 1.2 us)
Async XLA Ops:
  6.5 62.8 %copy-start = (bf16[512,1664]{1,0:T(8,128)(2,1)S(1)}, bf16[512,1664]{1,0:T(8,128)(2,1)}, u32[]{:S(2)}) copy-start(bf16[512,1664]{1,0:T(8,128)(2,1)} %param.8) | copy-start | bytes 5111812
  6.5 113.5 %all-gather.13.cloned.1.call-start = ((), (), s32[]{:S(2)}) async-start(), calls=%async_computation.4 | async-start | bytes 3311616 | tf_op jit(solution)/shard_map/all_gather | solution.py:55
  35.9 197.9 %all-gather.7.cloned.1.call-start = ((), (), s32[]{:S(2)}) async-start(), calls=%async_computation.1 | async-start | bytes 12300288 | tf_op jit(solution)/shard_map/all_gather | solution.py:47
  68.5 248.7 %all-gather.11.cloned.1.call-start = ((), (), s32[]{:S(2)}) async-start(), calls=%async_computation.3 | async-start | bytes 3514368 | tf_op jit(solution)/shard_map/all_gather | solution.py:62
  69.2 388.5 %all-gather.9.cloned.1.call-start = ((), (), s32[]{:S(2)}) async-start(), calls=%async_computation.2 | async-start | bytes 15335424 | tf_op jit(solution)/shard_map/all_gather | solution.py:64
  70.2 163.6 %copy-start.4 = (f32[1664]{0:T(1024)S(1)}, f32[1664]{0:T(1024)}, u32[]{:S(2)}) copy-start(f32[1664]{0:T(1024)} %param.9) | copy-start | bytes 19972
  254.9 4.3 copy-start.1
  266.5 2.7 copy-start.3
  269.2 1.8 copy-start.2
Sparse Core Ops, SparseCore 0:
  36.0 83.9 all-gather.12
  122.8 111.0 all-gather.6
  236.6 80.5 all-gather.10
  318.8 138.9 all-gather.8
where the time goes:
time: 525 us; the launch traced here: 521 us
  waiting for transfers between devices  329 us (63%)
  blocking collectives  97.3 us (19%)
  matrix products  37.7 us (7%)
  local copies, waits for them, and re-layouts  27.6 us (5%)
  other arithmetic  15.8 us (3%)
  between operations  13.4 us (3%)
    all_gather x1, waiting for transfers between devices, local(): lax.all_gather(merged, 'inner', axis=0, tiled=True)  141 us
    all_gather x1, waiting for transfers between devices, local(): lax.all_gather(qkv_part, 'dp', axis=1, tiled=True)  108 us
    all_gather x1, waiting for transfers between devices, local(): lax.all_gather(out_part, 'dp', axis=1, tiled=True)  47.9 us
    all_to_all x1, blocking collectives, local(): lax.all_to_all(outgoing, 'dp', split_axis=0, concat_axis=0, tiled=True)  38.8 us
    all_gather x1, waiting for transfers between devices, local(): merge_full = lax.all_gather(merge_weight, 'dp', axis=0, tiled=True)  32 us
    all_gather x1, blocking collectives, local(): qkv_part = lax.all_gather(qkv_weight, 'inner', axis=2, tiled=True)  29.9 us
    all_gather x1, blocking collectives, local(): out_part = lax.all_gather(out_weight, 'inner', axis=0, tiled=True)  28.6 us
    dot_general x1, matrix products, local(): jnp.einsum('td,cdh->cth', normed, lax.all_gather(qkv_part, 'dp', axis=1,...  12.2 us
  transfers between devices with their start and end apart: 4, of which 4 were waited for; matrix products, arithmetic and copies ran while one was open for 12% of the time, Pallas kernels for 0%

commit v1 on v0

--- a/solution.py
+++ b/solution.py
@@ -34,38 +34,52 @@
     return (shaped[0], shaped[1], shaped[2])
 
 
+def gather_weights(qkv_weight, out_weight, merge_weight):
+    n_dp = lax.axis_size("dp")
+    n_in = lax.axis_size("inner")
+    qkv_n = qkv_weight.size
+    out_n = out_weight.size
+    first = jnp.concatenate([qkv_weight.reshape(-1), out_weight.reshape(-1)])
+    first = lax.all_gather(first, "inner", axis=0, tiled=False)
+    second = jnp.concatenate([first.reshape(-1), merge_weight.reshape(-1)])
+    second = lax.all_gather(second, "dp", axis=0, tiled=False)
+    pair = second[:, : n_in * (qkv_n + out_n)].reshape(n_dp, n_in, qkv_n + out_n)
+    qkv_full = pair[:, :, :qkv_n].reshape((n_dp, n_in) + qkv_weight.shape)
+    out_full = pair[:, :, qkv_n:].reshape((n_dp, n_in) + out_weight.shape)
+    merge_full = second[:, n_in * (qkv_n + out_n) :].reshape(
+        (n_dp * merge_weight.shape[0], merge_weight.shape[1])
+    )
+    return qkv_full, out_full, merge_full
+
+
 def local(tokens, attn_gain, qkv_weight, out_weight, merge_gain, merge_weight, segment_ids, owners):
     tok_rows = tokens.shape[0]
+    n_dp = lax.axis_size("dp")
     local_segment = lax.dynamic_slice_in_dim(
         segment_ids, lax.axis_index("inner") * tok_rows, tok_rows
     )
+    qkv_full, out_full, merge_full = gather_weights(qkv_weight, out_weight, merge_weight)
     normed = layer_norm(tokens, attn_gain).astype(jnp.bfloat16)
-    qkv_part = lax.all_gather(qkv_weight, "inner", axis=2, tiled=True)
     projected = jnp.einsum(
-        "td,cdh->cth",
-        normed,
-        lax.all_gather(qkv_part, "dp", axis=1, tiled=True),
+        "tgk,gjcke->ctje",
+        normed.reshape(tok_rows, n_dp, -1),
+        qkv_full,
         preferred_element_type=jnp.float32,
-    )
-    queries, keys, vectors = split_heads(projected.astype(jnp.bfloat16))
-    context = attend_block(queries, keys, vectors, local_segment).reshape(tok_rows, -1)
-    out_part = lax.all_gather(out_weight, "inner", axis=0, tiled=True)
-    attn_out = jnp.dot(
-        context,
-        lax.all_gather(out_part, "dp", axis=1, tiled=True),
-        preferred_element_type=jnp.float32,
-    )
+    ).astype(jnp.bfloat16)
+    queries, keys, vectors = projected[0], projected[1], projected[2]
+    context = attend_block(queries, keys, vectors, local_segment)
+    attn_out = jnp.einsum(
+        "tje,gjek->tgk", context, out_full, preferred_element_type=jnp.float32
+    ).reshape(tok_rows, -1)
     hidden = tokens.astype(jnp.float32) + attn_out
     quad_rows = hidden.reshape(tok_rows // 4, -1)
     live = local_segment.reshape(-1, 4)[:, 0] >= 0
     merged = jnp.where(live[:, None], layer_norm(quad_rows, merge_gain), 0.0).astype(jnp.bfloat16)
-    merge_full = lax.all_gather(merge_weight, "dp", axis=0, tiled=True)
     features = jnp.dot(
         lax.all_gather(merged, "inner", axis=0, tiled=True),
         merge_full,
         preferred_element_type=jnp.float32,
     ).astype(jnp.bfloat16)
-    n_dp = lax.axis_size("dp")
     group_rows = features.shape[0]
     slots = 2 * group_rows // n_dp
     owner_col = owners[:, 0]

time: 525 us -> 490 us (0.933)
  waiting for transfers between devices: 329 us -> 238 us
  local copies, waits for them, and re-layouts: 27.6 us -> 107 us
  blocking collectives: 97.3 us -> 68.1 us
  other arithmetic: 15.8 us -> 26.3 us
  matrix products: 37.7 us -> 31.9 us
    all_gather x3 -> x1, waiting for transfers between devices: 188 us -> 118 us  [gather_weights(): second = lax.all_gather(second, 'dp', axis=0, tiled=False)]
    reshape x0 -> x6, local copies, waits for them, and re-layouts: none -> 36.6 us  [the longest x1 21.2 us: gather_weights(): qkv_full = pair[:, :, :qkv_n].reshape((n_dp, n_in) + qkv_weight.shape)]
    all_gather x2 -> x1, blocking collectives: 58.4 us -> 29.3 us  [gather_weights(): first = lax.all_gather(first, 'inner', axis=0, tiled=False)]
    all_gather x1, waiting for transfers between devices: 141 us -> 120 us  [local(): lax.all_gather(merged, 'inner', axis=0, tiled=True)]
    slice x3 -> x8, local copies, waits for them, and re-layouts: 1.35 us -> 16.1 us  [the longest x1 7.12 us: gather_weights(): qkv_full = pair[:, :, :qkv_n].reshape((n_dp, n_in) + qkv_weight.shape)]
    all_gather x2 -> x1, local copies, waits for them, and re-layouts: 1.74 us -> 13.1 us  [gather_weights(): second = lax.all_gather(second, 'dp', axis=0, tiled=False)]
    dot_general x0 -> x2, local copies, waits for them, and re-layouts: none -> 9.89 us  [the longest x1 8.27 us: local(): jnp.einsum('tje,gjek->tgk', context, out_full, preferred_element_type=jnp...]
    sub x1 -> x0, matrix products: 7.78 us -> none  [attend_block(): weights = jnp.exp(scores - top)]
  transfers between devices with their start and end apart: 4 -> 2, of which waited for: 4 -> 2; matrix products, arithmetic and copies ran while one was open for 12% -> 5% of each run, Pallas kernels for 0% -> 0%
where the time goes in v1:
time: 490 us; the launch traced here: 486 us
  waiting for transfers between devices  238 us (49%)
  local copies, waits for them, and re-layouts  107 us (22%)
  blocking collectives  68.1 us (14%)
  matrix products  31.9 us (7%)
  other arithmetic  26.3 us (5%)
  between operations  13.7 us (3%)
    all_gather x1, waiting for transfers between devices, local(): lax.all_gather(merged, 'inner', axis=0, tiled=True)  120 us
    all_gather x1, waiting for transfers between devices, gather_weights(): second = lax.all_gather(second, 'dp', axis=0, tiled=False)  118 us
    all_to_all x1, blocking collectives, local(): lax.all_to_all(outgoing, 'dp', split_axis=0, concat_axis=0, tiled=True)  38.8 us
    all_gather x1, blocking collectives, gather_weights(): first = lax.all_gather(first, 'inner', axis=0, tiled=False)  29.3 us
    reshape x1, local copies, waits for them, and re-layouts, gather_weights(): qkv_full = pair[:, :, :qkv_n].reshape((n_dp, n_in) + qkv_weight.shape)  21.2 us
    all_gather x1, local copies, waits for them, and re-layouts, gather_weights(): second = lax.all_gather(second, 'dp', axis=0, tiled=False)  13.1 us
    unnamed x20, local copies, waits for them, and re-layouts  12.9 us
    dot_general x1, matrix products, local(): jnp.einsum('tgk,gjcke->ctje', normed.reshape(tok_rows, n_dp, -1), qkv_ful...  10.3 us
  transfers between devices with their start and end apart: 2, of which 2 were waited for; matrix products, arithmetic and copies ran while one was open for 5% of the time, Pallas kernels for 0%

profile of v1, /device:TPU:30, one launch (start us, length us, event | category | flops | bytes accessed | tf_op | source)
XLA Modules:
  0.0 486.0 jit_solution(1451015235247029624)
XLA Ops:
  8.7 1.0 copy.36
  9.6 29.3 %all-gather.2 = bf16[8,1,21632]{2,1,0:T(2,128)(2,1)S(1)} all-gather(bf16[1,1,21632]{2,1,0:T(2,128)(2,1)S(1)} %reshape.144), channel_id=2, replica_groups=mesh['dp'=32,'inner'=8] {'inner'}, dimensions={0}, use_global_device_ids=true | all-gather | bytes 389376 | tf_op jit(solution)/shard_map/all_gather | solution.py:43
  39.0 2.1 reduce.5
  44.3 1.8 fusion.12
  46.0 2.8 copy.26
  48.9 1.4 reshape.146
  51.4 118.1 %all-gather.8.cloned.1.call-done = bf16[7241728]{0:T(1024)(128)(2,1)} async-done(((bf16[226304]{0:T(1024)(128)(2,1)}), bf16[7241728]{0:T(1024)(128)(2,1)}) %all-gather.8.cloned.1.call-update) | async-done | bytes 14483472 | tf_op jit(solution)/shard_map/all_gather | solution.py:45
  169.4 13.1 %reshape.141 = bf16[32,226304]{1,0:T(8,128)(2,1)} reshape(bf16[7241728]{0:T(1024)(128)(2,1)} %all-gather.8.cloned.1.call-done) | data formatting | bytes 28966912 | tf_op jit(solution)/shard_map/all_gather | solution.py:45
  182.6 4.1 slice-done
  186.7 5.3 %copy.37 = bf16[4,8,8,21632]{3,2,1,0:T(8,128)(2,1)S(1)} copy(bf16[4,8,8,21632]{3,1,2,0:T(8,128)(2,1)S(1)} %bitcast.66) | data formatting | bytes 22151168
  192.0 4.0 copy-done
  196.1 2.6 slice.48
  198.7 7.1 %slice.44 = bf16[32,8,16224]{2,1,0:T(8,128)(2,1)} slice(bf16[32,8,21632]{2,1,0:T(8,128)(2,1)} %bitcast.68), slice={[0:32], [0:8], [0:16224]} | slice | bytes 16613376 | tf_op jit(solution)/shard_map/slice | solution.py:47
  205.9 21.2 %reshape.118 = bf16[32,8,3,52,104]{4,3,2,1,0:T(8,128)(2,1)} reshape(bf16[32,8,16224]{2,1,0:T(8,128)(2,1)} %slice.44) | data formatting | bytes 16613376 | tf_op jit(solution)/shard_map/reshape | solution.py:47
  227.1 10.3 %fusion.1 = bf16[8,3,104,512,1]{3,2,0,1,4:T(8,128)(2,1)S(1)} fusion(bf16[32,8,3,52,104]{4,3,2,1,0:T(8,128)(2,1)} %reshape.118, bf16[512,32,52,1,1]{0,2,1,3,4:T(8,128)(2,1)S(1)} %copy-done.2), kind=kOutput, calls=%fused_computation.3 | convolution fusion | flops 4253024256 | bytes 12566528 | tf_op jit(solution)/shard_map/tgk,gjcke->ctje/dot_general | solution.py:63
  237.4 1.6 copy.51
  239.1 9.8 %reshape.120 = bf16[32,8,104,52]{3,2,1,0:T(8,128)(2,1)} reshape(bf16[32,8,5408]{2,1,0:T(8,128)(2,1)} %slice.48) | data formatting | bytes 5537792 | tf_op jit(solution)/shard_map/reshape | solution.py:48
  248.9 8.3 %copy.28 = bf16[32,52,104,8]{2,3,1,0:T(8,128)(2,1)} copy(bf16[32,52,104,8]{1,2,3,0:T(8,128)(2,1)} %bitcast.69) | data formatting | bytes 5537792 | tf_op jit(solution)/shard_map/tje,gjek->tgk/dot_general | solution.py:71
  257.2 2.7 fusion.21
  259.9 5.9 %fusion.32 = (f32[8,512]{1,0:T(8,128)S(1)}, f32[8,512,512]{1,2,0:T(8,128)}) fusion(f32[8,512,512]{1,2,0:T(8,128)S(1)} %fusion.21, pred[512,512]{0,1:T(8,128)(4,1)S(1)} %copy-done.3), kind=kOutput, calls=%fused_computation.59 | output fusion | flops 12583423 | bytes 17055744 | tf_op jit(solution)/shard_map/sub | solution.py:26
  265.9 9.3 %fusion.33 = (f32[512]{0:T(512)S(1)}, f32[512,1664]{1,0:T(8,128)}) fusion(bf16[1664,104,8]{1,2,0:T(8,128)(2,1)} %bitcast.74, f32[8,512,512]{1,2,0:T(8,128)} %get-tuple-element.6, f32[8,512]{1,0:T(8,128)S(1)} %get-tuple-element.5, bf16[3,512,8,104]{1,3,0,2:T(8,128)(2,1)} %bitcast.71, bf16[512,1664]{1,0:T(8,128)(2,1)S(1)} %copy-done.1), kind=kOutput, calls=%fused_computation.60 | convolution fusion | flops 1861058048 | bytes 17778688 | tf_op jit(solution)/shard_map/tje,gjek->tgk/dot_general | solution.py:71
  275.6 2.9 reshape.121
  278.5 2.4 multiply_reduce_fusion
  281.3 1.8 select_convert_fusion
  283.1 9.0 %reduce-window.6 = s32[32,8,128]{2,1,0:T(8,128)S(1)} reduce-window(s32[32,8,128]{2,1,0:T(8,128)S(1)} %fusion.25, s32[]{:T(128)} %constant.18.clone.1), window={size=1x1x128 pad=0_0x0_0x127_0}, to_apply=%region_8.9 | reduce-window | flops 4161536 | bytes 262148 | tf_op jit(solution)/shard_map/reduce-window
  292.7 4.3 scatter_custom_fusion
  297.0 2.0 slice-done.1
  299.0 3.0 reshape.122
  302.0 120.4 %all-gather.6.cloned.1.call-done = bf16[1024,6656]{1,0:T(8,128)(2,1)} async-done(((bf16[128,6656]{1,0:T(8,128)(2,1)}), bf16[1024,6656]{1,0:T(8,128)(2,1)}) %all-gather.6.cloned.1.call-update) | async-done | bytes 13631504 | tf_op jit(solution)/shard_map/all_gather | solution.py:79
  422.3 9.5 %convolution_convert_fusion = bf16[1024,256]{1,0:T(8,128)(2,1)S(1)} fusion(bf16[1024,6656]{1,0:T(8,128)(2,1)} %all-gather.6.cloned.1.call-done, bf16[6656,256]{1,0:T(8,128)(2,1)} %reshape.122), kind=kOutput, calls=%fused_computation.30 | convolution fusion | flops 3489923072 | bytes 17563648 | tf_op jit(solution)/shard_map/dot_general | solution.py:78
  431.9 7.5 %gather_fusion = bf16[2048,256]{1,0:T(8,128)(2,1)S(1)} fusion(bf16[1025,256]{1,0:T(8,128)(2,1)S(1)} %concatenate.11, s32[2048]{0:T(1024)S(1)} %fusion.27), kind=kCustom, calls=%fused_computation | custom fusion | bytes 2105344 | tf_op jit(solution)/shard_map/gather | solution.py:96
  439.4 38.8 %all_to_all.12 = bf16[32,64,256]{2,1,0:T(8,128)(2,1)S(1)} all-to-all(bf16[32,64,256]{2,1,0:T(8,128)(2,1)S(1)} %bitcast.73), channel_id=1, replica_groups=mesh['dp'=32,'inner'=8] {'dp'}, dimensions={0} | all-to-all | bytes 2097152 | tf_op jit(solution)/shard_map/all_to_all | solution.py:97
  (55 shorter events, 8.5 us)
Async XLA Ops:
  6.5 36.8 %copy-start.1 = (bf16[512,1664]{1,0:T(8,128)(2,1)S(1)}, bf16[512,1664]{1,0:T(8,128)(2,1)}, u32[]{:S(2)}) copy-start(bf16[512,1664]{1,0:T(8,128)(2,1)} %param.8) | copy-start | bytes 5111812
  6.5 162.9 %all-gather.8.cloned.1.call-start = ((), (), s32[]{:S(2)}) async-start(), calls=%async_computation.2 | async-start | bytes 14936064 | tf_op jit(solution)/shard_map/all_gather | solution.py:45
  39.0 5.3 %copy-start.6 = (f32[1664]{0:T(1024)S(1)}, f32[1664]{0:T(1024)}, u32[]{:S(2)}) copy-start(f32[1664]{0:T(1024)} %param.9) | copy-start | bytes 19972
  42.4 379.9 %all-gather.6.cloned.1.call-start = ((), (), s32[]{:S(2)}) async-start(), calls=%async_computation.1 | async-start | bytes 15335424 | tf_op jit(solution)/shard_map/all_gather | solution.py:79
  182.6 4.1 slice-start
  192.0 4.1 copy-start
  205.8 21.2 %copy-start.2 = (bf16[512,32,52,1,1]{0,2,1,3,4:T(8,128)(2,1)S(1)}, bf16[512,32,52,1,1]{0,2,1,3,4:T(8,128)(2,1)}, u32[]{:S(2)}) copy-start(bf16[512,32,52,1,1]{0,2,1,3,4:T(8,128)(2,1)} %reshape.146) | copy-start | bytes 5111812
  257.2 2.7 copy-start.3
  278.5 2.7 copy-start.5
  281.2 1.8 copy-start.4
  297.0 2.0 slice-start.1
Sparse Core Ops, SparseCore 0:
  42.5 126.8 all-gather.7
  283.2 139.0 all-gather.5

commit v2 on v0

--- a/solution.py
+++ b/solution.py
@@ -34,38 +34,53 @@
     return (shaped[0], shaped[1], shaped[2])
 
 
+def round8(rows):
+    return -(-rows // 8) * 8
+
+
+def pad_rows(block):
+    return jnp.pad(block, ((0, round8(block.shape[0]) - block.shape[0]), (0, 0)))
+
+
+def gather_weights(qkv_weight, out_weight):
+    slabs = [pad_rows(qkv_weight[c]) for c in range(3)] + [pad_rows(out_weight.T)]
+    stacked = jnp.concatenate(slabs, axis=0)
+    stacked = lax.all_gather(stacked, "inner", axis=1, tiled=True)
+    stacked = lax.all_gather(stacked, "dp", axis=0, tiled=False)
+    return stacked.reshape(stacked.shape[0], 4, -1, stacked.shape[-1])
+
+
 def local(tokens, attn_gain, qkv_weight, out_weight, merge_gain, merge_weight, segment_ids, owners):
     tok_rows = tokens.shape[0]
+    n_dp = lax.axis_size("dp")
     local_segment = lax.dynamic_slice_in_dim(
         segment_ids, lax.axis_index("inner") * tok_rows, tok_rows
     )
+    gathered = gather_weights(qkv_weight, out_weight)
     normed = layer_norm(tokens, attn_gain).astype(jnp.bfloat16)
-    qkv_part = lax.all_gather(qkv_weight, "inner", axis=2, tiled=True)
+    normed = normed.reshape(tok_rows, n_dp, -1)
+    normed = jnp.pad(normed, ((0, 0), (0, 0), (0, round8(normed.shape[-1]) - normed.shape[-1])))
     projected = jnp.einsum(
-        "td,cdh->cth",
+        "tgk,gckh->cth",
         normed,
-        lax.all_gather(qkv_part, "dp", axis=1, tiled=True),
+        gathered[:, :3],
         preferred_element_type=jnp.float32,
+    ).astype(jnp.bfloat16)
+    queries, keys, vectors = split_heads(projected)
+    context = attend_block(queries, keys, vectors, local_segment).reshape(tok_rows, -1)
+    attn_out = jnp.einsum(
+        "tf,gkf->tgk", context, gathered[:, 3], preferred_element_type=jnp.float32
     )
-    queries, keys, vectors = split_heads(projected.astype(jnp.bfloat16))
-    context = attend_block(queries, keys, vectors, local_segment).reshape(tok_rows, -1)
-    out_part = lax.all_gather(out_weight, "inner", axis=0, tiled=True)
-    attn_out = jnp.dot(
-        context,
-        lax.all_gather(out_part, "dp", axis=1, tiled=True),
-        preferred_element_type=jnp.float32,
-    )
+    attn_out = attn_out[:, :, : tokens.shape[1] // n_dp].reshape(tok_rows, -1)
     hidden = tokens.astype(jnp.float32) + attn_out
     quad_rows = hidden.reshape(tok_rows // 4, -1)
     live = local_segment.reshape(-1, 4)[:, 0] >= 0
     merged = jnp.where(live[:, None], layer_norm(quad_rows, merge_gain), 0.0).astype(jnp.bfloat16)
-    merge_full = lax.all_gather(merge_weight, "dp", axis=0, tiled=True)
     features = jnp.dot(
         lax.all_gather(merged, "inner", axis=0, tiled=True),
-        merge_full,
+        lax.all_gather(merge_weight, "dp", axis=0, tiled=True),
         preferred_element_type=jnp.float32,
     ).astype(jnp.bfloat16)
-    n_dp = lax.axis_size("dp")
     group_rows = features.shape[0]
     slots = 2 * group_rows // n_dp
     owner_col = owners[:, 0]

time: 525 us -> 449 us (0.86)
  waiting for transfers between devices: 329 us -> 269 us
  blocking collectives: 97.3 us -> 67.5 us
  local copies, waits for them, and re-layouts: 27.6 us -> 39.7 us
    all_gather x3 -> x2, waiting for transfers between devices: 188 us -> 128 us  [the longest x1 112 us: gather_weights(): stacked = lax.all_gather(stacked, 'dp', axis=0, tiled=False)]
    all_gather x2 -> x1, blocking collectives: 58.4 us -> 28.7 us  [gather_weights(): stacked = lax.all_gather(stacked, 'inner', axis=1, tiled=True)]
    reshape x0 -> x2, local copies, waits for them, and re-layouts: none -> 6.09 us  [the longest x1 4.68 us: local(): attn_out = attn_out[:, :, :tokens.shape[1] // n_dp].reshape(tok_rows, -1)]
  transfers between devices with their start and end apart: 4 -> 3, of which waited for: 4 -> 3; matrix products, arithmetic and copies ran while one was open for 12% -> 17% of each run, Pallas kernels for 0% -> 0%
where the time goes in v2:
time: 449 us; the launch traced here: 446 us
  waiting for transfers between devices  269 us (60%)
  blocking collectives  67.5 us (15%)
  local copies, waits for them, and re-layouts  39.7 us (9%)
  matrix products  35.1 us (8%)
  other arithmetic  20.4 us (5%)
  between operations  13.3 us (3%)
    all_gather x1, waiting for transfers between devices, local(): lax.all_gather(merged, 'inner', axis=0, tiled=True)  141 us
    all_gather x1, waiting for transfers between devices, gather_weights(): stacked = lax.all_gather(stacked, 'dp', axis=0, tiled=False)  112 us
    all_to_all x1, blocking collectives, local(): lax.all_to_all(outgoing, 'dp', split_axis=0, concat_axis=0, tiled=True)  38.8 us
    all_gather x1, blocking collectives, gather_weights(): stacked = lax.all_gather(stacked, 'inner', axis=1, tiled=True)  28.7 us
    all_gather x1, waiting for transfers between devices, local(): lax.all_gather(merge_weight, 'dp', axis=0, tiled=True)  15.6 us
    dot_general x1, matrix products, local(): jnp.einsum('tgk,gckh->cth', normed, gathered[:, :3], preferred_element_ty...  9.58 us
    dot_general x1, matrix products, local(): jnp.dot(lax.all_gather(merged, 'inner', axis=0, tiled=True), lax.all_gath...  9.51 us
    another operation x3, other arithmetic  9.15 us
  transfers between devices with their start and end apart: 3, of which 3 were waited for; matrix products, arithmetic and copies ran while one was open for 17% of the time, Pallas kernels for 0%

profile of v2, /device:TPU:30, one launch (start us, length us, event | category | flops | bytes accessed | tf_op | source)
XLA Modules:
  0.0 445.6 jit_solution(5642169367282242000)
XLA Ops:
  6.5 0.9 copy.29
  7.5 0.8 fusion.41
  8.7 28.7 %all_gather.15 = bf16[224,832]{0,1:T(8,128)(2,1)S(1)} all-gather(bf16[224,104]{0,1:T(8,128)(2,1)S(1)} %fusion.31), channel_id=1, replica_groups=mesh['dp'=32,'inner'=8] {'inner'}, dimensions={1}, use_global_device_ids=true | all-gather | bytes 419328 | tf_op jit(solution)/shard_map/all_gather | solution.py:48
  37.4 0.9 copy.30
  38.4 0.7 all-gather.7.cloned.1.call-update
  39.1 0.8 dynamic_slice.3
  40.0 0.9 broadcast_compare_fusion
  41.1 1.4 copy.25
  42.8 0.5 fusion.8
  43.3 0.5 fusion.10
  43.8 1.4 reshape.104
  45.3 112.3 %all-gather.9.cloned.1.call-done = bf16[7168,832]{1,0:T(8,128)(2,1)} async-done(((bf16[224,832]{1,0:T(8,128)(2,1)}), bf16[7168,832]{1,0:T(8,128)(2,1)}) %all-gather.9.cloned.1.call-update) | async-done | bytes 11927568 | tf_op jit(solution)/shard_map/all_gather | solution.py:49
  157.6 9.6 %fusion.13 = bf16[3,512,832]{1,2,0:T(8,128)(2,1)S(1)} fusion(bf16[32,4,56,832]{3,2,1,0:T(8,128)(2,1)} %bitcast.74, bf16[512,32,52]{0,2,1:T(8,128)(2,1)} %reshape.104), kind=kOutput, calls=%fused_computation.25 | convolution fusion | flops 4581457920 | bytes 16187392 | tf_op jit(solution)/shard_map/tgk,gckh->cth/dot_general | solution.py:63
  167.2 1.1 fusion.40
  168.3 3.8 slice_bitcast_fusion
  172.2 7.8 %fusion.42 = (f32[8,512]{1,0:T(8,128)S(1)}, f32[8,512,512]{1,2,0:T(8,128)}) fusion(pred[512,512]{0,1:T(8,128)(4,1)} %broadcast_compare_fusion, bf16[512,8,104]{0,2,1:T(8,128)(2,1)} %bitcast.73, bf16[512,8,104]{0,2,1:T(8,128)(2,1)S(1)} %bitcast.72), kind=kOutput, calls=%fused_computation.72 | convolution fusion | flops 444596736 | bytes 10371072 | tf_op jit(solution)/shard_map/sub | solution.py:26
  179.9 4.3 fusion.16
  184.3 3.9 fusion.11
  188.2 4.7 %reshape.106 = f32[512,1664]{0,1:T(8,128)} reshape(f32[512,32,52]{0,2,1:T(8,128)} %fusion.11) | data formatting | bytes 6815744 | tf_op jit(solution)/shard_map/reshape | solution.py:74
  192.9 4.2 fusion.39
  197.5 4.8 %copy.34 = f32[512,1664]{1,0:T(8,128)} copy(f32[512,1664]{0,1:T(8,128)} %get-tuple-element.6) | data formatting | bytes 6815744 | tf_op jit(solution)/shard_map/add | solution.py:75
  202.3 5.0 %reshape.107 = f32[128,6656]{1,0:T(8,128)} reshape(f32[512,1664]{1,0:T(8,128)} %copy.34) | data formatting | bytes 6815744 | tf_op jit(solution)/shard_map/reshape | solution.py:76
  207.3 0.4 multiply_reduce_fusion
  208.0 3.8 select_convert_fusion
  211.9 9.0 %reduce-window.6 = s32[32,8,128]{2,1,0:T(8,128)S(1)} reduce-window(s32[32,8,128]{2,1,0:T(8,128)S(1)} %fusion.22, s32[]{:T(128)} %constant.18.clone.1), window={size=1x1x128 pad=0_0x0_0x127_0}, to_apply=%region_8.9 | reduce-window | flops 4161536 | bytes 262148 | tf_op jit(solution)/shard_map/reduce-window
  221.5 4.3 scatter_custom_fusion
  225.8 15.6 %all-gather.7.cloned.1.call-done = bf16[6656,256]{1,0:T(8,128)(2,1)} async-done(((bf16[208,256]{1,0:T(8,128)(2,1)}), bf16[6656,256]{1,0:T(8,128)(2,1)}) %all-gather.7.cloned.1.call-update) | async-done | bytes 3407888 | tf_op jit(solution)/shard_map/all_gather | solution.py:81
  241.5 140.7 %all-gather.5.cloned.1.call-done = bf16[1024,6656]{1,0:T(8,128)(2,1)} async-done(((bf16[128,6656]{1,0:T(8,128)(2,1)}), bf16[1024,6656]{1,0:T(8,128)(2,1)}) %all-gather.5.cloned.1.call-update) | async-done | bytes 13631504 | tf_op jit(solution)/shard_map/all_gather | solution.py:80
  382.2 9.5 %convolution_convert_fusion = bf16[1024,256]{1,0:T(8,128)(2,1)S(1)} fusion(bf16[1024,6656]{1,0:T(8,128)(2,1)} %all-gather.5.cloned.1.call-done, bf16[6656,256]{1,0:T(8,128)(2,1)} %all-gather.7.cloned.1.call-done), kind=kOutput, calls=%fused_computation.29 | convolution fusion | flops 3489923072 | bytes 17563648 | tf_op jit(solution)/shard_map/dot_general | solution.py:79
  391.8 7.5 %gather_fusion = bf16[2048,256]{1,0:T(8,128)(2,1)S(1)} fusion(bf16[1025,256]{1,0:T(8,128)(2,1)S(1)} %concatenate.7, s32[2048]{0:T(1024)S(1)} %fusion.33), kind=kCustom, calls=%fused_computation | custom fusion | bytes 2105344 | tf_op jit(solution)/shard_map/gather | solution.py:97
  399.3 38.8 %all_to_all.12 = bf16[32,64,256]{2,1,0:T(8,128)(2,1)S(1)} all-to-all(bf16[32,64,256]{2,1,0:T(8,128)(2,1)S(1)} %bitcast.70), channel_id=1, replica_groups=mesh['dp'=32,'inner'=8] {'dp'}, dimensions={0} | all-to-all | bytes 2097152 | tf_op jit(solution)/shard_map/all_to_all | solution.py:98
  438.1 1.0 copy.47
  (46 shorter events, 2.4 us)
Async XLA Ops:
  6.5 34.5 %copy-start.2 = (bf16[512,1664]{1,0:T(8,128)(2,1)S(1)}, bf16[512,1664]{1,0:T(8,128)(2,1)}, u32[]{:S(2)}) copy-start(bf16[512,1664]{1,0:T(8,128)(2,1)} %param.8) | copy-start | bytes 5111812
  6.5 151.1 %all-gather.9.cloned.1.call-start = ((), (), s32[]{:S(2)}) async-start(), calls=%async_computation.3 | async-start | bytes 13246464 | tf_op jit(solution)/shard_map/all_gather | solution.py:49
  38.3 203.1 %all-gather.7.cloned.1.call-start = ((), (), s32[]{:S(2)}) async-start(), calls=%async_computation.2 | async-start | bytes 3514368 | tf_op jit(solution)/shard_map/all_gather | solution.py:81
  39.1 343.1 %all-gather.5.cloned.1.call-start = ((), (), s32[]{:S(2)}) async-start(), calls=%async_computation.1 | async-start | bytes 15335424 | tf_op jit(solution)/shard_map/all_gather | solution.py:80
  41.1 2.2 copy-start.5
  179.9 4.3 copy-start.1
  202.3 5.0 %copy-start = (f32[512,1664]{0,1:T(8,128)S(1)}, f32[512,1664]{0,1:T(8,128)}, u32[]{:S(2)}) copy-start(f32[512,1664]{0,1:T(8,128)} %get-tuple-element.6) | copy-start | bytes 10223620
  207.3 0.7 copy-start.4
  208.0 3.9 copy-start.3
Sparse Core Ops, SparseCore 0:
  38.5 119.0 all-gather.8
  160.4 81.0 all-gather.6
  243.3 138.8 all-gather.4

commit v3 on v2

--- a/solution.py
+++ b/solution.py
@@ -1,7 +1,7 @@
 import jax
 import jax.numpy as jnp
 from jax import lax
-from jax.sharding import PartitionSpec as P
+from jax.sharding import Mesh, PartitionSpec as P
 
 HEAD_DIM = 104
 
@@ -42,21 +42,28 @@
     return jnp.pad(block, ((0, round8(block.shape[0]) - block.shape[0]), (0, 0)))
 
 
+def gather_dp(block):
+    halves = lax.all_gather(block, "dq", axis=0, tiled=False)
+    whole = lax.all_gather(halves, "core", axis=1, tiled=False)
+    return whole.reshape((-1,) + block.shape)
+
+
 def gather_weights(qkv_weight, out_weight):
     slabs = [pad_rows(qkv_weight[c]) for c in range(3)] + [pad_rows(out_weight.T)]
     stacked = jnp.concatenate(slabs, axis=0)
     stacked = lax.all_gather(stacked, "inner", axis=1, tiled=True)
-    stacked = lax.all_gather(stacked, "dp", axis=0, tiled=False)
+    stacked = gather_dp(stacked)
     return stacked.reshape(stacked.shape[0], 4, -1, stacked.shape[-1])
 
 
 def local(tokens, attn_gain, qkv_weight, out_weight, merge_gain, merge_weight, segment_ids, owners):
     tok_rows = tokens.shape[0]
-    n_dp = lax.axis_size("dp")
+    n_dp = lax.axis_size("dq") * lax.axis_size("core")
     local_segment = lax.dynamic_slice_in_dim(
         segment_ids, lax.axis_index("inner") * tok_rows, tok_rows
     )
     gathered = gather_weights(qkv_weight, out_weight)
+    merge_weight, gathered = lax.optimization_barrier((merge_weight, gathered))
     normed = layer_norm(tokens, attn_gain).astype(jnp.bfloat16)
     normed = normed.reshape(tok_rows, n_dp, -1)
     normed = jnp.pad(normed, ((0, 0), (0, 0), (0, round8(normed.shape[-1]) - normed.shape[-1])))
@@ -78,7 +85,7 @@
     merged = jnp.where(live[:, None], layer_norm(quad_rows, merge_gain), 0.0).astype(jnp.bfloat16)
     features = jnp.dot(
         lax.all_gather(merged, "inner", axis=0, tiled=True),
-        lax.all_gather(merge_weight, "dp", axis=0, tiled=True),
+        gather_dp(merge_weight).reshape(-1, merge_weight.shape[1]),
         preferred_element_type=jnp.float32,
     ).astype(jnp.bfloat16)
     group_rows = features.shape[0]
@@ -95,20 +102,23 @@
     )
     padded = jnp.concatenate([features, jnp.zeros((1, features.shape[1]), jnp.bfloat16)], axis=0)
     outgoing = padded[source_row]
-    return lax.all_to_all(outgoing, "dp", split_axis=0, concat_axis=0, tiled=True)
+    return lax.all_to_all(outgoing, ("dq", "core"), split_axis=0, concat_axis=0, tiled=True)
 
 
 def solution(mesh):
+    dp = ("dq", "core")
+    n_dp, n_in = mesh.shape["dp"], mesh.shape["inner"]
+    split = Mesh(mesh.devices.reshape(n_dp // 2, 2, n_in), ("dq", "core", "inner"))
     placed = (
-        P(("dp", "inner"), None),
+        P((*dp, "inner"), None),
         P(),
-        P(None, "dp", "inner"),
-        P("inner", "dp"),
+        P(None, dp, "inner"),
+        P("inner", dp),
         P(),
-        P("dp", "inner"),
-        P("dp"),
-        P("dp", None),
+        P(dp, "inner"),
+        P(dp),
+        P(dp, None),
     )
     return jax.shard_map(
-        local, mesh=mesh, in_specs=placed, out_specs=P("dp", "inner"), check_vma=False
+        local, mesh=split, in_specs=placed, out_specs=P(dp, "inner"), check_vma=False
     )

time: 449 us -> 508 us (1.13)
  waiting for transfers between devices: 269 us -> 326 us
    all_gather x2 -> x4, waiting for transfers between devices: 128 us -> 201 us  [the longest x2 176 us: gather_dp(): halves = lax.all_gather(block, 'dq', axis=0, tiled=False)]
    all_gather x1, waiting for transfers between devices: 141 us -> 125 us  [local(): lax.all_gather(merged, 'inner', axis=0, tiled=True)]
  transfers between devices with their start and end apart: 3 -> 5, of which waited for: 3 -> 4; matrix products, arithmetic and copies ran while one was open for 17% -> 15% of each run, Pallas kernels for 0% -> 0%
where the time goes in v3:
time: 508 us; the launch traced here: 504 us
  waiting for transfers between devices  326 us (64%)
  blocking collectives  67.5 us (13%)
  local copies, waits for them, and re-layouts  39.5 us (8%)
  matrix products  36.7 us (7%)
  other arithmetic  20.7 us (4%)
  between operations  13.4 us (3%)
    all_gather x2, waiting for transfers between devices, gather_dp(): halves = lax.all_gather(block, 'dq', axis=0, tiled=False)  176 us
    all_gather x1, waiting for transfers between devices, local(): lax.all_gather(merged, 'inner', axis=0, tiled=True)  125 us
    all_to_all x1, blocking collectives, local(): lax.all_to_all(outgoing, ('dq', 'core'), split_axis=0, concat_axis=0, til...  38.8 us
    all_gather x1, blocking collectives, gather_weights(): stacked = lax.all_gather(stacked, 'inner', axis=1, tiled=True)  28.7 us
    all_gather x2, waiting for transfers between devices, gather_dp(): whole = lax.all_gather(halves, 'core', axis=1, tiled=False)  24.4 us
  transfers between devices with their start and end apart: 5, of which 4 were waited for; matrix products, arithmetic and copies ran while one was open for 15% of the time, Pallas kernels for 0%

profile of v3, /device:TPU:30, one launch (start us, length us, event | category | flops | bytes accessed | tf_op | source)
XLA Modules:
  0.0 504.2 jit_solution(7431344735082021506)
XLA Ops:
  6.5 0.8 copy.41
  7.4 0.8 fusion.41
  8.6 28.7 %all_gather.30 = bf16[224,832]{0,1:T(8,128)(2,1)S(1)} all-gather(bf16[224,104]{0,1:T(8,128)(2,1)S(1)} %fusion.31), channel_id=1, replica_groups=mesh['dq'=16,'core'=2,'inner'=8] {'inner'}, dimensions={1}, use_global_device_ids=true | all-gather | bytes 419328 | tf_op jit(solution)/shard_map/all_gather | solution.py:54
  37.2 0.9 copy.42
  38.3 117.7 %all-gather.12.cloned.1.call-done = bf16[3584,832]{1,0:T(8,128)(2,1)} async-done(((bf16[224,832]{1,0:T(8,128)(2,1)}), bf16[3584,832]{1,0:T(8,128)(2,1)}) %all-gather.12.cloned.1.call-update) | async-done | bytes 5963792 | tf_op jit(solution)/shard_map/all_gather | solution.py:46
  156.0 0.8 dynamic_slice.3
  156.9 1.4 copy.37
  158.6 0.5 fusion.8
  159.2 0.5 fusion.10
  159.7 1.4 reshape.100
  161.2 0.9 broadcast_compare_fusion
  162.1 24.4 %all-gather.14.cloned.1.call-done = bf16[16,448,832]{2,1,0:T(8,128)(2,1)} async-done(((bf16[16,224,832]{2,1,0:T(8,128)(2,1)}), bf16[16,448,832]{2,1,0:T(8,128)(2,1)}) %all-gather.14.cloned.1.call-update) | async-done | bytes 11927568 | tf_op jit(solution)/shard_map/all_gather | solution.py:47
  186.8 9.6 %fusion.13 = bf16[3,512,832]{1,2,0:T(8,128)(2,1)S(1)} fusion(bf16[32,4,56,832]{3,2,1,0:T(8,128)(2,1)} %bitcast.77, bf16[512,32,52]{0,2,1:T(8,128)(2,1)} %reshape.100), kind=kOutput, calls=%fused_computation.25 | convolution fusion | flops 4581457920 | bytes 16187392 | tf_op jit(solution)/shard_map/tgk,gckh->cth/dot_general | solution.py:70
  196.4 1.1 fusion.40
  197.5 3.8 slice_bitcast_fusion
  201.3 7.7 %fusion.42 = (f32[8,512]{1,0:T(8,128)S(1)}, f32[8,512,512]{1,2,0:T(8,128)}) fusion(pred[512,512]{0,1:T(8,128)(4,1)} %broadcast_compare_fusion, bf16[512,8,104]{0,2,1:T(8,128)(2,1)} %bitcast.76, bf16[512,8,104]{0,2,1:T(8,128)(2,1)S(1)} %bitcast.75), kind=kOutput, calls=%fused_computation.72 | convolution fusion | flops 444596736 | bytes 10371072 | tf_op jit(solution)/shard_map/sub | solution.py:26
  209.0 4.2 fusion.16
  213.2 58.6 %all-gather.16.cloned.1.call-done = bf16[3328,256]{1,0:T(8,128)(2,1)} async-done(((bf16[208,256]{1,0:T(8,128)(2,1)}), bf16[3328,256]{1,0:T(8,128)(2,1)}) %all-gather.16.cloned.1.call-update) | async-done | bytes 1703952 | tf_op jit(solution)/shard_map/all_gather | solution.py:46
  272.0 5.8 %fusion.11 = f32[512,32,52]{0,2,1:T(8,128)} fusion(bf16[512,832,1]{0,1,2:T(8,128)(2,1)S(1)} %bitcast.90, bf16[32,56,832]{2,1,0:T(8,128)(2,1)} %slice_bitcast_fusion), kind=kOutput, calls=%fused_computation.22 | convolution fusion | flops 1417674752 | bytes 7241728 | tf_op jit(solution)/shard_map/tf,gkf->tgk/dot_general | solution.py:78
  277.8 4.6 reshape.102
  282.4 4.6 fusion.39
  287.5 4.8 copy.46
  292.3 4.9 reshape.103
  297.2 0.4 multiply_reduce_fusion
  298.0 3.8 select_convert_fusion
  301.8 9.0 %reduce-window.6 = s32[32,8,128]{2,1,0:T(8,128)S(1)} reduce-window(s32[32,8,128]{2,1,0:T(8,128)S(1)} %fusion.22, s32[]{:T(128)} %constant.18.clone.1), window={size=1x1x128 pad=0_0x0_0x127_0}, to_apply=%region_8.9 | reduce-window | flops 4161536 | bytes 262148 | tf_op jit(solution)/shard_map/reduce-window
  311.3 4.3 scatter_custom_fusion
  315.7 125.1 %all-gather.10.cloned.1.call-done = bf16[1024,6656]{1,0:T(8,128)(2,1)} async-done(((bf16[128,6656]{1,0:T(8,128)(2,1)}), bf16[1024,6656]{1,0:T(8,128)(2,1)}) %all-gather.10.cloned.1.call-update) | async-done | bytes 13631504 | tf_op jit(solution)/shard_map/all_gather | solution.py:87
  440.8 9.5 %convolution_convert_fusion = bf16[1024,256]{1,0:T(8,128)(2,1)S(1)} fusion(bf16[1024,6656]{1,0:T(8,128)(2,1)} %all-gather.10.cloned.1.call-done, bf16[6656,256]{1,0:T(8,128)(2,1)} %bitcast.89), kind=kOutput, calls=%fused_computation.29 | convolution fusion | flops 3489923072 | bytes 17563648 | tf_op jit(solution)/shard_map/dot_general | solution.py:86
  450.4 7.5 %gather_fusion = bf16[2048,256]{1,0:T(8,128)(2,1)S(1)} fusion(bf16[1025,256]{1,0:T(8,128)(2,1)S(1)} %concatenate.7, s32[2048]{0:T(1024)S(1)} %fusion.33), kind=kCustom, calls=%fused_computation | custom fusion | bytes 2105344 | tf_op jit(solution)/shard_map/gather | solution.py:104
  457.9 38.8 %all_to_all.12 = bf16[32,64,256]{2,1,0:T(8,128)(2,1)S(1)} all-to-all(bf16[32,64,256]{2,1,0:T(8,128)(2,1)S(1)} %bitcast.72), channel_id=1, replica_groups=mesh['dq'=16,'core'=2,'inner'=8] {'dq','core'}, dimensions={0} | all-to-all | bytes 2097152 | tf_op jit(solution)/shard_map/all_to_all | solution.py:105
  496.7 1.0 copy.59
  (50 shorter events, 2.9 us)
Async XLA Ops:
  6.5 149.4 %all-gather.12.cloned.1.call-start = ((), (), s32[]{:S(2)}) async-start(), calls=%async_computation.2 | async-start | bytes 6823936 | tf_op jit(solution)/shard_map/all_gather | solution.py:46
  38.2 118.7 %copy-start.1 = (bf16[512,1664]{1,0:T(8,128)(2,1)S(1)}, bf16[512,1664]{1,0:T(8,128)(2,1)}, u32[]{:S(2)}) copy-start(bf16[512,1664]{1,0:T(8,128)(2,1)} %param.8) | copy-start | bytes 5111812
  38.2 148.3 %all-gather.14.cloned.1.call-start = ((), (), s32[]{:S(2)}) async-start(), calls=%async_computation.3 | async-start | bytes 19267584 | tf_op jit(solution)/shard_map/all_gather | solution.py:47
  156.0 115.8 %all-gather.16.cloned.1.call-start = ((), (), s32[]{:S(2)}) async-start(), calls=%async_computation.4 | async-start | bytes 1810432 | tf_op jit(solution)/shard_map/all_gather | solution.py:46
  156.9 2.2 copy-start.4
  186.6 129.1 %all-gather.18.cloned.1.call-start = ((), (), s32[]{:S(2)}) async-start(), calls=%async_computation.5 | async-start | bytes 5111808 | tf_op jit(solution)/shard_map/all_gather | solution.py:47
  271.8 169.0 %all-gather.10.cloned.1.call-start = ((), (), s32[]{:S(2)}) async-start(), calls=%async_computation.1 | async-start | bytes 15335424 | tf_op jit(solution)/shard_map/all_gather | solution.py:87
  292.3 4.9 copy-start
  297.2 0.7 copy-start.3
  298.0 3.8 copy-start.2
Sparse Core Ops, SparseCore 0:
  38.3 117.5 all-gather.11
  157.8 28.7 all-gather.13
  189.1 82.5 all-gather.15
  273.4 15.9 all-gather.17
  301.9 138.8 all-gather.9

commit v4 on v2

--- a/solution.py
+++ b/solution.py
@@ -42,11 +42,17 @@
     return jnp.pad(block, ((0, round8(block.shape[0]) - block.shape[0]), (0, 0)))
 
 
+def gather_a2a(block, axis):
+    count = lax.axis_size(axis)
+    copies = jnp.broadcast_to(block[None], (count,) + block.shape)
+    return lax.all_to_all(copies, axis, split_axis=0, concat_axis=0, tiled=True)
+
+
 def gather_weights(qkv_weight, out_weight):
     slabs = [pad_rows(qkv_weight[c]) for c in range(3)] + [pad_rows(out_weight.T)]
     stacked = jnp.concatenate(slabs, axis=0)
     stacked = lax.all_gather(stacked, "inner", axis=1, tiled=True)
-    stacked = lax.all_gather(stacked, "dp", axis=0, tiled=False)
+    stacked = gather_a2a(stacked, "dp")
     return stacked.reshape(stacked.shape[0], 4, -1, stacked.shape[-1])
 
 
@@ -77,7 +83,7 @@
     live = local_segment.reshape(-1, 4)[:, 0] >= 0
     merged = jnp.where(live[:, None], layer_norm(quad_rows, merge_gain), 0.0).astype(jnp.bfloat16)
     features = jnp.dot(
-        lax.all_gather(merged, "inner", axis=0, tiled=True),
+        gather_a2a(merged, "inner").reshape(-1, merged.shape[1]),
         lax.all_gather(merge_weight, "dp", axis=0, tiled=True),
         preferred_element_type=jnp.float32,
     ).astype(jnp.bfloat16)

time: 449 us -> 665 us (1.48)
  waiting for transfers between devices: 269 us -> 461 us
  starting transfers between devices: 0.08 us -> 18.1 us
  local copies, waits for them, and re-layouts: 39.7 us -> 51 us
    all_to_all x0 -> x2, waiting for transfers between devices: none -> 276 us  [gather_a2a(): return lax.all_to_all(copies, axis, split_axis=0, concat_axis=0, tiled=True)]
    all_gather x2 -> x0, waiting for transfers between devices: 253 us -> none  [the longest x1 141 us: local(): lax.all_gather(merged, 'inner', axis=0, tiled=True)]
    all_gather x1, waiting for transfers between devices: 15.6 us -> 184 us  [local(): lax.all_gather(merge_weight, 'dp', axis=0, tiled=True)]
    all_to_all x0 -> x2, starting transfers between devices: none -> 18.1 us  [gather_a2a(): return lax.all_to_all(copies, axis, split_axis=0, concat_axis=0, tiled=True)]
    broadcast_in_dim x0 -> x2, local copies, waits for them, and re-layouts: none -> 11.6 us  [gather_a2a(): copies = jnp.broadcast_to(block[None], (count,) + block.shape)]
  transfers between devices with their start and end apart: 3 -> 3, of which waited for: 3 -> 3; matrix products, arithmetic and copies ran while one was open for 17% -> 3% of each run, Pallas kernels for 0% -> 0%
where the time goes in v4:
time: 665 us; the launch traced here: 664 us
  waiting for transfers between devices  461 us (69%)
  blocking collectives  66 us (10%)
  local copies, waits for them, and re-layouts  51 us (8%)
  matrix products  34.7 us (5%)
  other arithmetic  19.9 us (3%)
  starting transfers between devices  18.1 us (3%)
  between operations  13.7 us (2%)
    all_to_all x2, waiting for transfers between devices, gather_a2a(): return lax.all_to_all(copies, axis, split_axis=0, concat_axis=0, tiled=True)  276 us
    all_gather x1, waiting for transfers between devices, local(): lax.all_gather(merge_weight, 'dp', axis=0, tiled=True)  184 us
    all_to_all x1, blocking collectives, local(): lax.all_to_all(outgoing, 'dp', split_axis=0, concat_axis=0, tiled=True)  37.4 us
    all_gather x1, blocking collectives, gather_weights(): stacked = lax.all_gather(stacked, 'inner', axis=1, tiled=True)  28.7 us
    all_to_all x2, starting transfers between devices, gather_a2a(): return lax.all_to_all(copies, axis, split_axis=0, concat_axis=0, tiled=True)  18.1 us
  transfers between devices with their start and end apart: 3, of which 3 were waited for; matrix products, arithmetic and copies ran while one was open for 3% of the time, Pallas kernels for 0%

profile of v4, /device:TPU:30, one launch (start us, length us, event | category | flops | bytes accessed | tf_op | source)
XLA Modules:
  0.0 663.9 jit_solution(6970321728048307072)
XLA Ops:
  6.5 0.8 copy.29
  7.4 0.8 fusion.41
  8.6 28.7 %all_gather.6 = bf16[224,832]{0,1:T(8,128)(2,1)S(1)} all-gather(bf16[224,104]{0,1:T(8,128)(2,1)S(1)} %fusion.31), channel_id=1, replica_groups=mesh['dp'=32,'inner'=8] {'inner'}, dimensions={1}, use_global_device_ids=true | all-gather | bytes 419328 | tf_op jit(solution)/shard_map/all_gather | solution.py:54
  37.5 5.5 broadcast_in_dim.36
  43.0 11.8 %all-to-all-start = ((bf16[32,224,832]{2,1,0:T(8,128)(2,1)}), bf16[32,224,832]{2,1,0:T(8,128)(2,1)}, u32[]{:S(2)}, u32[]{:S(2)}) async-start(bf16[32,224,832]{2,1,0:T(8,128)(2,1)} %broadcast_in_dim.36), calls=%async_computation | async-start | bytes 25690112 | tf_op jit(solution)/shard_map/all_to_all | solution.py:48
  54.8 1.4 copy.25
  57.6 1.4 reshape.168
  59.0 0.8 dynamic_slice.3
  60.5 0.9 fusion.29
  61.5 0.9 broadcast_compare_fusion
  62.4 270.8 %all-to-all-done = bf16[32,224,832]{2,1,0:T(8,128)(2,1)} async-done(((bf16[32,224,832]{2,1,0:T(8,128)(2,1)}), bf16[32,224,832]{2,1,0:T(8,128)(2,1)}, u32[]{:S(2)}, u32[]{:S(2)}) %all-to-all-start) | async-done | bytes 11927584 | tf_op jit(solution)/shard_map/all_to_all | solution.py:48
  333.2 3.8 slice_bitcast_fusion
  337.0 9.3 %fusion.13 = bf16[3,512,832]{1,2,0:T(8,128)(2,1)S(1)} fusion(bf16[32,4,56,832]{3,2,1,0:T(8,128)(2,1)} %bitcast.4, bf16[512,32,52]{0,2,1:T(8,128)(2,1)S(1)} %copy-done.2), kind=kOutput, calls=%fused_computation.25 | convolution fusion | flops 4581457920 | bytes 16187392 | tf_op jit(solution)/shard_map/tgk,gckh->cth/dot_general | solution.py:69
  346.4 1.1 fusion.40
  347.5 7.7 %fusion.42 = (f32[8,512]{1,0:T(8,128)S(1)}, f32[8,512,512]{1,2,0:T(8,128)}) fusion(pred[512,512]{0,1:T(8,128)(4,1)} %broadcast_compare_fusion, bf16[512,8,104]{0,2,1:T(8,128)(2,1)} %bitcast.73, bf16[512,8,104]{0,2,1:T(8,128)(2,1)S(1)} %bitcast.72), kind=kOutput, calls=%fused_computation.72 | convolution fusion | flops 444596736 | bytes 10371072 | tf_op jit(solution)/shard_map/sub | solution.py:26
  355.2 4.3 fusion.16
  359.5 3.9 fusion.11
  363.3 4.6 reshape.170
  368.0 4.2 fusion.39
  372.2 4.8 copy.34
  377.0 4.9 reshape.171
  383.0 2.6 select_convert_fusion
  385.6 6.1 broadcast_in_dim.40
  391.6 6.3 all-to-all-start.1
  398.7 9.0 %reduce-window.6 = s32[32,8,128]{2,1,0:T(8,128)S(1)} reduce-window(s32[32,8,128]{2,1,0:T(8,128)S(1)} %fusion.22, s32[]{:T(128)} %constant.18.clone.1), window={size=1x1x128 pad=0_0x0_0x127_0}, to_apply=%region_8.9 | reduce-window | flops 4161536 | bytes 262148 | tf_op jit(solution)/shard_map/reduce-window
  408.3 4.3 scatter_custom_fusion
  412.6 183.7 %all-gather.2.cloned.1.call-done = bf16[6656,256]{1,0:T(8,128)(2,1)} async-done(((bf16[208,256]{1,0:T(8,128)(2,1)}), bf16[6656,256]{1,0:T(8,128)(2,1)}) %all-gather.2.cloned.1.call-update) | async-done | bytes 3407888 | tf_op jit(solution)/shard_map/all_gather | solution.py:87
  596.3 5.4 all-to-all-done.1
  601.7 9.5 %convolution_convert_fusion = bf16[1024,256]{1,0:T(8,128)(2,1)S(1)} fusion(bf16[1024,6656]{1,0:T(8,128)(2,1)} %bitcast.16, bf16[6656,256]{1,0:T(8,128)(2,1)} %all-gather.2.cloned.1.call-done), kind=kOutput, calls=%fused_computation.29 | convolution fusion | flops 3489923072 | bytes 17563648 | tf_op jit(solution)/shard_map/dot_general | solution.py:85
  611.3 7.5 %gather_fusion = bf16[2048,256]{1,0:T(8,128)(2,1)S(1)} fusion(bf16[1025,256]{1,0:T(8,128)(2,1)S(1)} %concatenate.7, s32[2048]{0:T(1024)S(1)} %fusion.33), kind=kCustom, calls=%fused_computation | custom fusion | bytes 2105344 | tf_op jit(solution)/shard_map/gather | solution.py:103
  618.8 37.4 %all_to_all.22 = bf16[32,64,256]{2,1,0:T(8,128)(2,1)S(1)} all-to-all(bf16[32,64,256]{2,1,0:T(8,128)(2,1)S(1)} %bitcast.70), channel_id=1, replica_groups=mesh['dp'=32,'inner'=8] {'dp'}, dimensions={0} | all-to-all | bytes 2097152 | tf_op jit(solution)/shard_map/all_to_all | solution.py:104
  656.1 1.0 copy.47
  (48 shorter events, 5.1 us)
Async XLA Ops:
  43.0 11.8 %copy-start.3 = (bf16[512,1664]{1,0:T(8,128)(2,1)S(1)}, bf16[512,1664]{1,0:T(8,128)(2,1)}, u32[]{:S(2)}) copy-start(bf16[512,1664]{1,0:T(8,128)(2,1)} %param.8) | copy-start | bytes 5111812
  43.0 290.2 %all-to-all-start = ((bf16[32,224,832]{2,1,0:T(8,128)(2,1)}), bf16[32,224,832]{2,1,0:T(8,128)(2,1)}, u32[]{:S(2)}, u32[]{:S(2)}) async-start(bf16[32,224,832]{2,1,0:T(8,128)(2,1)} %broadcast_in_dim.36), calls=%async_computation | async-start | bytes 25690112 | tf_op jit(solution)/shard_map/all_to_all | solution.py:48
  54.8 2.2 copy-start.6
  59.8 277.3 %copy-start.2 = (bf16[512,32,52]{0,2,1:T(8,128)(2,1)S(1)}, bf16[512,32,52]{0,2,1:T(8,128)(2,1)}, u32[]{:S(2)}) copy-start(bf16[512,32,52]{0,2,1:T(8,128)(2,1)} %reshape.168) | copy-start | bytes 5111812
  355.2 4.3 copy-start.1
  377.0 5.4 copy-start
  381.9 1.1 copy-start.5
  391.6 7.0 %copy-start.4 = (s32[1024,1]{0,1:T(1,128)S(1)}, s32[1024,1]{0,1:T(1,128)}, u32[]{:S(2)}) copy-start(s32[1024,1]{0,1:T(1,128)} %param.15) | copy-start | bytes 12292
  391.6 210.1 %all-to-all-start.1 = ((bf16[8,128,6656]{2,1,0:T(8,128)(2,1)}), bf16[8,128,6656]{2,1,0:T(8,128)(2,1)}, u32[]{:S(2)}, u32[]{:S(2)}) async-start(bf16[8,128,6656]{2,1,0:T(8,128)(2,1)} %broadcast_in_dim.40), calls=%async_computation.1 | async-start | bytes 27262976 | tf_op jit(solution)/shard_map/all_to_all | solution.py:48
  398.0 198.3 %all-gather.2.cloned.1.call-start = ((), (), s32[]{:S(2)}) async-start(), calls=%async_computation.3 | async-start | bytes 3514368 | tf_op jit(solution)/shard_map/all_gather | solution.py:87
Sparse Core Ops, SparseCore 0:
  401.5 194.7 all-gather.1

commit v5 on v2

--- a/solution.py
+++ b/solution.py
@@ -42,34 +42,53 @@
     return jnp.pad(block, ((0, round8(block.shape[0]) - block.shape[0]), (0, 0)))
 
 
-def gather_weights(qkv_weight, out_weight):
-    slabs = [pad_rows(qkv_weight[c]) for c in range(3)] + [pad_rows(out_weight.T)]
-    stacked = jnp.concatenate(slabs, axis=0)
-    stacked = lax.all_gather(stacked, "inner", axis=1, tiled=True)
-    stacked = lax.all_gather(stacked, "dp", axis=0, tiled=False)
-    return stacked.reshape(stacked.shape[0], 4, -1, stacked.shape[-1])
+def owner_rows(owners, n_dp, group_rows):
+    slots = 2 * group_rows // n_dp
+    owner_col = owners[:, 0]
+    chosen = (owner_col[:, None] == jnp.arange(n_dp, dtype=jnp.int32)[None, :]).astype(jnp.int32)
+    earlier = jnp.cumsum(chosen, axis=0) - chosen
+    rank = jnp.sum(earlier * chosen, axis=1)
+    target = owner_col * slots + rank
+    return (
+        jnp.full((n_dp * slots,), group_rows, jnp.int32)
+        .at[target]
+        .set(jnp.arange(group_rows, dtype=jnp.int32))
+    )
 
 
 def local(tokens, attn_gain, qkv_weight, out_weight, merge_gain, merge_weight, segment_ids, owners):
     tok_rows = tokens.shape[0]
     n_dp = lax.axis_size("dp")
+    n_in = lax.axis_size("inner")
+    lanes = n_in * qkv_weight.shape[-1]
     local_segment = lax.dynamic_slice_in_dim(
         segment_ids, lax.axis_index("inner") * tok_rows, tok_rows
     )
-    gathered = gather_weights(qkv_weight, out_weight)
+    slabs = [pad_rows(qkv_weight[c]) for c in range(3)] + [pad_rows(out_weight.T)]
+    stacked = lax.all_gather(jnp.concatenate(slabs, axis=0), "inner", axis=1, tiled=True)
+    merge_rows = -(-merge_weight.size // lanes)
+    flat = jnp.pad(merge_weight.reshape(-1), (0, merge_rows * lanes - merge_weight.size))
+    payload = jnp.concatenate([stacked, flat.reshape(merge_rows, lanes)], axis=0)
+    gathered = lax.all_gather(payload, "dp", axis=0, tiled=False)
+    owners, payload = lax.optimization_barrier((owners, payload))
+    source_row = owner_rows(owners, n_dp, n_in * tok_rows // 4)
+    source_row, tokens = lax.optimization_barrier((source_row, tokens))
+    weights = gathered[:, : stacked.shape[0]].reshape(n_dp, 4, -1, lanes)
+    merge_full = gathered[:, stacked.shape[0] :].reshape(n_dp, -1)[:, : merge_weight.size]
+    merge_full = merge_full.reshape(-1, merge_weight.shape[1])
     normed = layer_norm(tokens, attn_gain).astype(jnp.bfloat16)
     normed = normed.reshape(tok_rows, n_dp, -1)
     normed = jnp.pad(normed, ((0, 0), (0, 0), (0, round8(normed.shape[-1]) - normed.shape[-1])))
     projected = jnp.einsum(
         "tgk,gckh->cth",
         normed,
-        gathered[:, :3],
+        weights[:, :3],
         preferred_element_type=jnp.float32,
     ).astype(jnp.bfloat16)
     queries, keys, vectors = split_heads(projected)
     context = attend_block(queries, keys, vectors, local_segment).reshape(tok_rows, -1)
     attn_out = jnp.einsum(
-        "tf,gkf->tgk", context, gathered[:, 3], preferred_element_type=jnp.float32
+        "tf,gkf->tgk", context, weights[:, 3], preferred_element_type=jnp.float32
     )
     attn_out = attn_out[:, :, : tokens.shape[1] // n_dp].reshape(tok_rows, -1)
     hidden = tokens.astype(jnp.float32) + attn_out
@@ -78,23 +97,12 @@
     merged = jnp.where(live[:, None], layer_norm(quad_rows, merge_gain), 0.0).astype(jnp.bfloat16)
     features = jnp.dot(
         lax.all_gather(merged, "inner", axis=0, tiled=True),
-        lax.all_gather(merge_weight, "dp", axis=0, tiled=True),
+        merge_full,
         preferred_element_type=jnp.float32,
     ).astype(jnp.bfloat16)
     group_rows = features.shape[0]
-    slots = 2 * group_rows // n_dp
-    owner_col = owners[:, 0]
-    chosen = (owner_col[:, None] == jnp.arange(n_dp, dtype=jnp.int32)[None, :]).astype(jnp.int32)
-    earlier = jnp.cumsum(chosen, axis=0) - chosen
-    rank = jnp.sum(earlier * chosen, axis=1)
-    target = owner_col * slots + rank
-    source_row = (
-        jnp.full((n_dp * slots,), group_rows, jnp.int32)
-        .at[target]
-        .set(jnp.arange(group_rows, dtype=jnp.int32))
-    )
-    padded = jnp.concatenate([features, jnp.zeros((1, features.shape[1]), jnp.bfloat16)], axis=0)
-    outgoing = padded[source_row]
+    pick = (source_row[:, None] == jnp.arange(group_rows, dtype=jnp.int32)[None, :]).astype(jnp.bfloat16)
+    outgoing = jnp.dot(pick, features, preferred_element_type=jnp.float32).astype(jnp.bfloat16)
     return lax.all_to_all(outgoing, "dp", split_axis=0, concat_axis=0, tiled=True)
 
 

time: 449 us -> 431 us (0.960)
  waiting for transfers between devices: 269 us -> 245 us
  local copies, waits for them, and re-layouts: 39.7 us -> 47.7 us
    all_gather x1, waiting for transfers between devices: 141 us -> 128 us  [local(): lax.all_gather(merged, 'inner', axis=0, tiled=True)]
    all_gather x2 -> x1, waiting for transfers between devices: 128 us -> 117 us  [local(): gathered = lax.all_gather(payload, 'dp', axis=0, tiled=False)]
    slice x3 -> x5, local copies, waits for them, and re-layouts: 0.97 us -> 11.5 us  [the longest x1 6.36 us: local(): weights = gathered[:, :stacked.shape[0]].reshape(n_dp, 4, -1, lanes)]
    gather x1 -> x0, local copies, waits for them, and re-layouts: 7.5 us -> none  [local(): outgoing = padded[source_row]]
    another operation x2 -> x3, local copies, waits for them, and re-layouts: 0.08 us -> 7.04 us  [the longest x1 6.96 us: local(): merge_full = merge_full.reshape(-1, merge_weight.shape[1])]
  transfers between devices with their start and end apart: 3 -> 2, of which waited for: 3 -> 2; matrix products, arithmetic and copies ran while one was open for 17% -> 7% of each run, Pallas kernels for 0% -> 0%
where the time goes in v5:
time: 431 us; the launch traced here: 427 us
  waiting for transfers between devices  245 us (57%)
  blocking collectives  67.7 us (16%)
  local copies, waits for them, and re-layouts  47.7 us (11%)
  matrix products  34.6 us (8%)
  other arithmetic  18.5 us (4%)
  between operations  13.7 us (3%)
    all_gather x1, waiting for transfers between devices, local(): lax.all_gather(merged, 'inner', axis=0, tiled=True)  128 us
    all_gather x1, waiting for transfers between devices, local(): gathered = lax.all_gather(payload, 'dp', axis=0, tiled=False)  117 us
    all_to_all x1, blocking collectives, local(): lax.all_to_all(outgoing, 'dp', split_axis=0, concat_axis=0, tiled=True)  39 us
    all_gather x1, blocking collectives, local(): lax.all_gather(jnp.concatenate(slabs, axis=0), 'inner', axis=1, tiled=True)  28.7 us
    dot_general x1, matrix products, local(): jnp.dot(pick, features, preferred_element_type=jnp.float32)  12.7 us
    another operation x3, other arithmetic  9.15 us
  transfers between devices with their start and end apart: 2, of which 2 were waited for; matrix products, arithmetic and copies ran while one was open for 7% of the time, Pallas kernels for 0%

profile of v5, /device:TPU:30, one launch (start us, length us, event | category | flops | bytes accessed | tf_op | source)
XLA Modules:
  0.0 427.4 jit_solution(15866131090154614850)
XLA Ops:
  6.5 0.9 copy.53
  7.5 0.8 fusion.43
  8.6 1.1 reshape.108
  10.0 28.7 %all_gather.12 = bf16[224,832]{0,1:T(8,128)(2,1)S(1)} all-gather(bf16[224,104]{0,1:T(8,128)(2,1)S(1)} %fusion.34), channel_id=1, replica_groups=mesh['dp'=32,'inner'=8] {'inner'}, dimensions={1}, use_global_device_ids=true | all-gather | bytes 419328 | tf_op jit(solution)/shard_map/all_gather | solution.py:68
  38.8 1.1 copy.58
  40.0 0.8 dynamic_slice.3
  40.9 9.0 %reduce-window.6 = s32[32,8,128]{2,1,0:T(8,128)S(1)} reduce-window(s32[32,8,128]{2,1,0:T(8,128)S(1)} %fusion.25, s32[]{:T(128)} %constant.18.clone.1), window={size=1x1x128 pad=0_0x0_0x127_0}, to_apply=%region_0.1 | reduce-window | flops 4161536 | bytes 262148 | tf_op jit(solution)/shard_map/reduce-window
  50.4 4.5 %scatter_custom_fusion = s32[2048]{0:T(1024)S(1)} fusion(s32[1024]{0:T(1024)S(1)} %bitcast.88, s32[1024]{0:T(1024)S(1)} %iota.15, s32[]{:T(128)} %constant.15.clone.1), kind=kCustom, calls=%fused_computation.62 | custom fusion | bytes 8196 | tf_op jit(solution)/shard_map/scatter | solution.py:55
  54.9 1.4 copy.57
  56.6 0.5 fusion.10
  57.2 0.5 fusion.12
  57.7 1.4 reshape.112
  59.2 0.9 broadcast_compare_fusion
  60.1 117.0 %all-gather.6.cloned.1.call-done = bf16[9216,832]{1,0:T(8,128)(2,1)} async-done(((bf16[288,832]{1,0:T(8,128)(2,1)}), bf16[9216,832]{1,0:T(8,128)(2,1)}) %all-gather.6.cloned.1.call-update) | async-done | bytes 15335440 | tf_op jit(solution)/shard_map/all_gather | solution.py:72
  177.1 6.4 %slice.63 = bf16[32,224,832]{2,1,0:T(8,128)(2,1)S(1)} slice(bf16[32,288,832]{2,1,0:T(8,128)(2,1)} %bitcast.72), slice={[0:32], [0:224], [0:832]} | slice | bytes 23855104 | tf_op jit(solution)/shard_map/slice | solution.py:76
  183.5 2.0 slice_bitcast_fusion
  185.6 6.2 %fusion.16 = bf16[3,512,832]{1,2,0:T(8,128)(2,1)S(1)} fusion(bf16[32,4,56,832]{3,2,1,0:T(8,128)(2,1)S(1)} %bitcast.71, bf16[512,32,52]{0,2,1:T(8,128)(2,1)S(1)} %copy-done.2), kind=kOutput, calls=%fused_computation.28 | convolution fusion | flops 4581457920 | bytes 16187392 | tf_op jit(solution)/shard_map/tgk,gckh->cth/dot_general | solution.py:82
  191.8 1.1 fusion.42
  192.9 7.6 %fusion.44 = (f32[8,512]{1,0:T(8,128)S(1)}, f32[8,512,512]{1,2,0:T(8,128)}) fusion(pred[512,512]{0,1:T(8,128)(4,1)} %broadcast_compare_fusion, bf16[512,8,104]{0,2,1:T(8,128)(2,1)} %bitcast.78, bf16[512,8,104]{0,2,1:T(8,128)(2,1)S(1)} %bitcast.77), kind=kOutput, calls=%fused_computation.74 | convolution fusion | flops 444596736 | bytes 10371072 | tf_op jit(solution)/shard_map/sub | solution.py:26
  200.6 4.3 %fusion.19 = bf16[8,104,512]{2,1,0:T(8,128)(2,1)S(1)} fusion(bf16[512,8,104]{0,2,1:T(8,128)(2,1)S(1)} %bitcast.76, f32[8,512,512]{1,2,0:T(8,128)} %get-tuple-element.20, f32[8,512]{1,0:T(8,128)S(1)} %get-tuple-element.19), kind=kOutput, calls=%fused_computation.31 | convolution fusion | flops 440827904 | bytes 10108928 | tf_op jit(solution)/shard_map/hqk,khe->qhe/dot_general | solution.py:28
  204.9 3.9 fusion.13
  208.7 4.7 %reshape.114 = f32[512,1664]{0,1:T(8,128)} reshape(f32[512,32,52]{0,2,1:T(8,128)} %fusion.13) | data formatting | bytes 6815744 | tf_op jit(solution)/shard_map/reshape | solution.py:93
  213.4 4.2 fusion.41
  218.1 5.2 %copy.62 = f32[512,1664]{1,0:T(8,128)} copy(f32[512,1664]{0,1:T(8,128)} %get-tuple-element.12) | data formatting | bytes 6815744 | tf_op jit(solution)/shard_map/add | solution.py:94
  223.7 2.9 reshape.115
  226.8 1.8 select_convert_fusion
  228.6 4.1 slice.69
  232.8 7.0 %reshape_reshape.3 = bf16[6656,256]{1,0:T(8,128)(2,1)S(1)} reshape(bf16[32,64,832]{2,1,0:T(8,128)(2,1)} %slice.69) | data formatting | bytes 6815744 | tf_op jit(solution)/shard_map/reshape;reshape | solution.py:78
  239.7 128.1 %all-gather.4.cloned.1.call-done = bf16[1024,6656]{1,0:T(8,128)(2,1)} async-done(((bf16[128,6656]{1,0:T(8,128)(2,1)}), bf16[1024,6656]{1,0:T(8,128)(2,1)}) %all-gather.4.cloned.1.call-update) | async-done | bytes 13631504 | tf_op jit(solution)/shard_map/all_gather | solution.py:99
  367.9 12.7 %fusion.15 = bf16[2048,256]{1,0:T(8,128)(2,1)} fusion(s32[2048]{0:T(1024)S(1)} %scatter_custom_fusion, bf16[1024,6656]{1,0:T(8,128)(2,1)} %all-gather.4.cloned.1.call-done, bf16[6656,256]{1,0:T(8,128)(2,1)S(1)} %reshape_reshape.3), kind=kOutput, calls=%fused_computation.27 | convolution fusion | flops 4566286336 | bytes 18096128 | tf_op jit(solution)/shard_map/dot_general | solution.py:105
  380.5 39.0 %all_to_all.12 = bf16[32,64,256]{2,1,0:T(8,128)(2,1)S(1)} all-to-all(bf16[32,64,256]{2,1,0:T(8,128)(2,1)} %bitcast.75), channel_id=1, replica_groups=mesh['dp'=32,'inner'=8] {'dp'}, dimensions={0} | all-to-all | bytes 2097152 | tf_op jit(solution)/shard_map/all_to_all | solution.py:106
  419.6 1.0 copy.73
  (48 shorter events, 3.1 us)
Async XLA Ops:
  6.5 34.3 %copy-start.4 = (s32[1024,1]{0,1:T(1,128)S(1)}, s32[1024,1]{0,1:T(1,128)}, u32[]{:S(2)}) copy-start(s32[1024,1]{0,1:T(1,128)} %param.15) | copy-start | bytes 12292
  6.5 48.4 %copy-start.3 = (bf16[512,1664]{1,0:T(8,128)(2,1)S(1)}, bf16[512,1664]{1,0:T(8,128)(2,1)}, u32[]{:S(2)}) copy-start(bf16[512,1664]{1,0:T(8,128)(2,1)} %param.8) | copy-start | bytes 5111812
  6.5 170.6 %all-gather.6.cloned.1.call-start = ((), (), s32[]{:S(2)}) async-start(), calls=%async_computation.2 | async-start | bytes 17031168 | tf_op jit(solution)/shard_map/all_gather | solution.py:72
  39.9 328.0 %all-gather.4.cloned.1.call-start = ((), (), s32[]{:S(2)}) async-start(), calls=%async_computation.1 | async-start | bytes 15335424 | tf_op jit(solution)/shard_map/all_gather | solution.py:99
  54.9 2.2 copy-start.6
  183.5 2.2 copy-start.2
  200.6 4.3 %copy-start.1 = (bf16[32,56,832]{2,1,0:T(8,128)(2,1)S(1)}, bf16[32,56,832]{2,1,0:T(8,128)(2,1)}, u32[]{:S(2)}) copy-start(bf16[32,56,832]{2,1,0:T(8,128)(2,1)} %slice_bitcast_fusion) | copy-start | bytes 8945668
  218.0 5.2 %copy-start = (f32[512,1664]{0,1:T(8,128)S(1)}, f32[512,1664]{0,1:T(8,128)}, u32[]{:S(2)}) copy-start(f32[512,1664]{0,1:T(8,128)} %get-tuple-element.12) | copy-start | bytes 10223620
  223.7 3.2 copy-start.5
Sparse Core Ops, SparseCore 0:
  40.0 137.0 all-gather.5
  228.8 139.0 all-gather.3

commit v6 on v5

--- a/solution.py
+++ b/solution.py
@@ -66,16 +66,31 @@
     )
     slabs = [pad_rows(qkv_weight[c]) for c in range(3)] + [pad_rows(out_weight.T)]
     stacked = lax.all_gather(jnp.concatenate(slabs, axis=0), "inner", axis=1, tiled=True)
+    real = qkv_weight.shape[1]
+    tall = round8(real)
+    stacked = stacked.reshape(4, tall, lanes)
     merge_rows = -(-merge_weight.size // lanes)
     flat = jnp.pad(merge_weight.reshape(-1), (0, merge_rows * lanes - merge_weight.size))
-    payload = jnp.concatenate([stacked, flat.reshape(merge_rows, lanes)], axis=0)
+    flat = flat.reshape(merge_rows, lanes)
+    spare = min(4 * (tall - real), merge_rows)
+    if spare:
+        tail = flat[:spare].reshape(4, spare // 4, lanes)
+        tail = jnp.pad(tail, ((0, 0), (0, tall - real - spare // 4), (0, 0)))
+        stacked = jnp.concatenate([stacked[:, :real], tail], axis=1)
+    rest = flat[spare:]
+    extra = -(-rest.shape[0] // tall)
+    rest = jnp.pad(rest, ((0, extra * tall - rest.shape[0]), (0, 0))).reshape(extra, tall, lanes)
+    payload = jnp.concatenate([stacked, rest], axis=0)
     gathered = lax.all_gather(payload, "dp", axis=0, tiled=False)
     owners, payload = lax.optimization_barrier((owners, payload))
     source_row = owner_rows(owners, n_dp, n_in * tok_rows // 4)
     source_row, tokens = lax.optimization_barrier((source_row, tokens))
-    weights = gathered[:, : stacked.shape[0]].reshape(n_dp, 4, -1, lanes)
-    merge_full = gathered[:, stacked.shape[0] :].reshape(n_dp, -1)[:, : merge_weight.size]
-    merge_full = merge_full.reshape(-1, merge_weight.shape[1])
+    weights = gathered[:, :4]
+    merge_full = jnp.concatenate(
+        [gathered[:, :4, real:].reshape(n_dp, -1, lanes)[:, :spare], gathered[:, 4:].reshape(n_dp, -1, lanes)],
+        axis=1,
+    )
+    merge_full = merge_full.reshape(n_dp, -1)[:, : merge_weight.size].reshape(-1, merge_weight.shape[1])
     normed = layer_norm(tokens, attn_gain).astype(jnp.bfloat16)
     normed = normed.reshape(tok_rows, n_dp, -1)
     normed = jnp.pad(normed, ((0, 0), (0, 0), (0, round8(normed.shape[-1]) - normed.shape[-1])))
@@ -92,9 +107,15 @@
     )
     attn_out = attn_out[:, :, : tokens.shape[1] // n_dp].reshape(tok_rows, -1)
     hidden = tokens.astype(jnp.float32) + attn_out
-    quad_rows = hidden.reshape(tok_rows // 4, -1)
-    live = local_segment.reshape(-1, 4)[:, 0] >= 0
-    merged = jnp.where(live[:, None], layer_norm(quad_rows, merge_gain), 0.0).astype(jnp.bfloat16)
+    width = 4 * hidden.shape[1]
+    quad_sum = jnp.sum(hidden, axis=-1).reshape(-1, 4).sum(axis=-1)
+    center = hidden - jnp.repeat(quad_sum / width, 4)[:, None]
+    quad_sq = jnp.sum(center * center, axis=-1).reshape(-1, 4).sum(axis=-1)
+    scale = jnp.repeat(lax.rsqrt(quad_sq / width + EPS), 4)
+    gain = jnp.tile(merge_gain.reshape(4, -1), (tok_rows // 4, 1))
+    live = jnp.repeat(local_segment.reshape(-1, 4)[:, 0] >= 0, 4)
+    merged = jnp.where(live[:, None], center * scale[:, None] * gain, 0.0).astype(jnp.bfloat16)
+    merged = merged.reshape(tok_rows // 4, -1)
     features = jnp.dot(
         lax.all_gather(merged, "inner", axis=0, tiled=True),
         merge_full,

time: 431 us -> 428 us (level)
  waiting for transfers between devices: 245 us -> 222 us
  local copies, waits for them, and re-layouts: 47.7 us -> 58.4 us
  other arithmetic: 18.5 us -> 25.2 us
    reshape x4 -> x10, local copies, waits for them, and re-layouts: 4.26 us -> 20.3 us  [the longest x2 9.17 us: local(): merge_full.reshape(n_dp, -1)[:, :merge_weight.size]]
    all_gather x1, waiting for transfers between devices: 117 us -> 102 us  [local(): gathered = lax.all_gather(payload, 'dp', axis=0, tiled=False)]
    all_gather x1, waiting for transfers between devices: 128 us -> 119 us  [local(): lax.all_gather(merged, 'inner', axis=0, tiled=True)]
    reduce_sum x0 -> x4, other arithmetic: none -> 5.18 us  [the longest x2 2.69 us: local(): quad_sq = jnp.sum(center * center, axis=-1).reshape(-1, 4).sum(axis=-1)]
    add x1 -> x0, local copies, waits for them, and re-layouts: 5.18 us -> none  [local(): hidden = tokens.astype(jnp.float32) + attn_out]
    another operation x3 -> x6, local copies, waits for them, and re-layouts: 7.04 us -> 12.2 us  [the longest x4 12.1 us: local(): gain = jnp.tile(merge_gain.reshape(4, -1), (tok_rows // 4, 1))]
    slice x4 -> x8, local copies, waits for them, and re-layouts: 10.7 us -> 7.18 us  [the longest x1 3.07 us: local(): gathered[:, :4, real:].reshape(n_dp, -1, lanes)[:, :spare]]
  transfers between devices with their start and end apart: 2 -> 2, of which waited for: 2 -> 2; matrix products, arithmetic and copies ran while one was open for 7% -> 12% of each run, Pallas kernels for 0% -> 0%
where the time goes in v6:
time: 428 us; the launch traced here: 425 us
  waiting for transfers between devices  222 us (52%)
  blocking collectives  67.5 us (16%)
  local copies, waits for them, and re-layouts  58.4 us (14%)
  matrix products  38 us (9%)
  other arithmetic  25.2 us (6%)
  between operations  13.7 us (3%)
    all_gather x1, waiting for transfers between devices, local(): lax.all_gather(merged, 'inner', axis=0, tiled=True)  119 us
    all_gather x1, waiting for transfers between devices, local(): gathered = lax.all_gather(payload, 'dp', axis=0, tiled=False)  102 us
    all_to_all x1, blocking collectives, local(): lax.all_to_all(outgoing, 'dp', split_axis=0, concat_axis=0, tiled=True)  38.8 us
    all_gather x1, blocking collectives, local(): lax.all_gather(jnp.concatenate(slabs, axis=0), 'inner', axis=1, tiled=True)  28.7 us
    dot_general x1, matrix products, local(): jnp.dot(pick, features, preferred_element_type=jnp.float32)  12.7 us
    another operation x4, local copies, waits for them, and re-layouts, local(): gain = jnp.tile(merge_gain.reshape(4, -1), (tok_rows // 4, 1))  12.1 us
    dot_general x1, matrix products, local(): jnp.einsum('tgk,gckh->cth', normed, weights[:, :3], preferred_element_typ...  9.52 us
    reshape x2, local copies, waits for them, and re-layouts, local(): merge_full.reshape(n_dp, -1)[:, :merge_weight.size]  9.17 us
  transfers between devices with their start and end apart: 2, of which 2 were waited for; matrix products, arithmetic and copies ran while one was open for 12% of the time, Pallas kernels for 0%

profile of v6, /device:TPU:30, one launch (start us, length us, event | category | flops | bytes accessed | tf_op | source)
XLA Modules:
  0.0 424.5 jit_solution(7190352165980321605)
XLA Ops:
  10.6 28.7 %all_gather.12 = bf16[224,832]{0,1:T(8,128)(2,1)S(1)} all-gather(bf16[224,104]{0,1:T(8,128)(2,1)S(1)} %fusion.35), channel_id=1, replica_groups=mesh['dp'=32,'inner'=8] {'inner'}, dimensions={1}, use_global_device_ids=true | all-gather | bytes 419328 | tf_op jit(solution)/shard_map/all_gather | solution.py:68
  41.7 9.0 %reduce-window.6 = s32[32,8,128]{2,1,0:T(8,128)S(1)} reduce-window(s32[32,8,128]{2,1,0:T(8,128)S(1)} %fusion.26, s32[]{:T(128)} %constant.18.clone.1), window={size=1x1x128 pad=0_0x0_0x127_0}, to_apply=%region_0.1 | reduce-window | flops 4161536 | bytes 262148 | tf_op jit(solution)/shard_map/reduce-window
  51.3 4.3 %scatter_custom_fusion = s32[2048]{0:T(1024)S(1)} fusion(s32[1024]{0:T(1024)S(1)} %bitcast.93, s32[1024]{0:T(1024)S(1)} %iota.15, s32[]{:T(128)} %constant.15.clone.1), kind=kCustom, calls=%fused_computation.66 | custom fusion | bytes 8196 | tf_op jit(solution)/shard_map/scatter | solution.py:55
  55.6 1.4 copy.47
  58.4 1.4 reshape.131
  59.8 2.2 tile.11
  62.1 5.1 %tile.12 = f32[512,1664]{1,0:T(8,128)} reshape(f32[128,4,1664]{2,1,0:T(4,128)} %tile.11) | data formatting | bytes 6815744 | tf_op jit(solution)/shard_map/tile | solution.py:115
  67.1 4.8 %copy.51 = f32[512,1664]{0,1:T(8,128)} copy(f32[512,1664]{1,0:T(8,128)} %tile.12) | data formatting | bytes 6815744 | tf_op jit(solution)/shard_map/tile | solution.py:115
  71.9 0.9 broadcast_compare_fusion
  72.8 102.4 %all-gather.6.cloned.1.call-done = bf16[160,56,832]{2,1,0:T(8,128)(2,1)} async-done(((bf16[5,56,832]{2,1,0:T(8,128)(2,1)}), bf16[160,56,832]{2,1,0:T(8,128)(2,1)}) %all-gather.6.cloned.1.call-update) | async-done | bytes 14909456 | tf_op jit(solution)/shard_map/all_gather | solution.py:84
  175.2 6.2 %slice_bitcast_fusion = (bf16[32,56,832]{2,1,0:T(8,128)(2,1)}, bf16[32,56,832]{2,1,0:T(8,128)(2,1)}) fusion(bf16[32,5,56,832]{3,2,1,0:T(8,128)(2,1)} %bitcast.76), kind=kLoop, calls=%fused_computation.25 | loop fusion | bytes 11927552 | tf_op jit(solution)/shard_map/reshape | solution.py:90
  181.4 9.5 %fusion.16 = bf16[3,512,832]{1,2,0:T(8,128)(2,1)S(1)} fusion(bf16[32,5,56,832]{3,2,1,0:T(8,128)(2,1)} %bitcast.77, bf16[512,32,52]{0,2,1:T(8,128)(2,1)S(1)} %copy-done.2), kind=kOutput, calls=%fused_computation.30 | convolution fusion | flops 4581457920 | bytes 19169280 | tf_op jit(solution)/shard_map/tgk,gckh->cth/dot_general | solution.py:97
  191.0 1.1 fusion.42
  192.1 7.7 %fusion.44 = (f32[8,512]{1,0:T(8,128)S(1)}, f32[8,512,512]{1,2,0:T(8,128)}) fusion(pred[512,512]{0,1:T(8,128)(4,1)} %broadcast_compare_fusion, bf16[512,8,104]{0,2,1:T(8,128)(2,1)} %bitcast.83, bf16[512,8,104]{0,2,1:T(8,128)(2,1)S(1)} %bitcast.82), kind=kOutput, calls=%fused_computation.77 | convolution fusion | flops 444596736 | bytes 10371072 | tf_op jit(solution)/shard_map/sub | solution.py:26
  199.8 4.3 %fusion.19 = bf16[8,104,512]{2,1,0:T(8,128)(2,1)S(1)} fusion(bf16[512,8,104]{0,2,1:T(8,128)(2,1)S(1)} %bitcast.81, f32[8,512,512]{1,2,0:T(8,128)} %get-tuple-element.20, f32[8,512]{1,0:T(8,128)S(1)} %get-tuple-element.19), kind=kOutput, calls=%fused_computation.33 | convolution fusion | flops 440827904 | bytes 10108928 | tf_op jit(solution)/shard_map/hqk,khe->qhe/dot_general | solution.py:28
  204.1 3.9 fusion.13
  207.9 4.6 %reshape.133 = f32[512,1664]{0,1:T(8,128)} reshape(f32[512,32,52]{0,2,1:T(8,128)} %fusion.13) | data formatting | bytes 6815744 | tf_op jit(solution)/shard_map/reshape | solution.py:108
  212.6 2.4 fusion.20
  215.4 2.6 multiply_reduce_fusion
  218.4 4.0 select_convert_fusion
  222.5 1.4 copy.52
  223.9 2.1 reshape.136
  226.0 3.1 slice.93
  229.1 2.4 reshape.137
  231.4 3.4 pad_maximum_fusion
  234.9 6.2 %reshape.139 = bf16[32,59904]{1,0:T(8,128)(2,1)} reshape(bf16[32,72,832]{2,1,0:T(8,128)(2,1)} %pad_maximum_fusion) | data formatting | bytes 7667712 | tf_op jit(solution)/shard_map/reshape | solution.py:93
  241.0 2.0 slice-done
  243.0 3.0 reshape.140
  246.0 119.2 %all-gather.4.cloned.1.call-done = bf16[1024,6656]{1,0:T(8,128)(2,1)} async-done(((bf16[128,6656]{1,0:T(8,128)(2,1)}), bf16[1024,6656]{1,0:T(8,128)(2,1)}) %all-gather.4.cloned.1.call-update) | async-done | bytes 13631504 | tf_op jit(solution)/shard_map/all_gather | solution.py:120
  365.2 12.7 %fusion.15 = bf16[2048,256]{1,0:T(8,128)(2,1)S(1)} fusion(s32[2048]{0:T(1024)S(1)} %scatter_custom_fusion, bf16[1024,6656]{1,0:T(8,128)(2,1)} %all-gather.4.cloned.1.call-done, bf16[6656,256]{1,0:T(8,128)(2,1)} %reshape.140), kind=kOutput, calls=%fused_computation.29 | convolution fusion | flops 4566286336 | bytes 18096128 | tf_op jit(solution)/shard_map/dot_general | solution.py:126
  377.9 38.8 %all_to_all.12 = bf16[32,64,256]{2,1,0:T(8,128)(2,1)S(1)} all-to-all(bf16[32,64,256]{2,1,0:T(8,128)(2,1)S(1)} %bitcast.80), channel_id=1, replica_groups=mesh['dp'=32,'inner'=8] {'dp'}, dimensions={0} | all-to-all | bytes 2097152 | tf_op jit(solution)/shard_map/all_to_all | solution.py:127
  416.7 1.0 copy.63
  (63 shorter events, 9.1 us)
Async XLA Ops:
  6.5 33.9 %copy-start.5 = (f32[6656]{0:T(1024)S(1)}, f32[6656]{0:T(1024)}, u32[]{:S(2)}) copy-start(f32[6656]{0:T(1024)} %param.12) | copy-start | bytes 79876
  6.5 35.2 %copy-start.4 = (s32[1024,1]{0,1:T(1,128)S(1)}, s32[1024,1]{0,1:T(1,128)}, u32[]{:S(2)}) copy-start(s32[1024,1]{0,1:T(1,128)} %param.15) | copy-start | bytes 12292
  6.5 49.1 %copy-start.3 = (bf16[512,1664]{1,0:T(8,128)(2,1)S(1)}, bf16[512,1664]{1,0:T(8,128)(2,1)}, u32[]{:S(2)}) copy-start(bf16[512,1664]{1,0:T(8,128)(2,1)} %param.8) | copy-start | bytes 5111812
  6.5 168.7 %all-gather.6.cloned.1.call-start = ((), (), s32[]{:S(2)}) async-start(), calls=%async_computation.2 | async-start | bytes 16558080 | tf_op jit(solution)/shard_map/all_gather | solution.py:84
  40.4 324.8 %all-gather.4.cloned.1.call-start = ((), (), s32[]{:S(2)}) async-start(), calls=%async_computation.1 | async-start | bytes 15335424 | tf_op jit(solution)/shard_map/all_gather | solution.py:120
  55.6 2.2 copy-start.6
  175.2 6.2 %copy-start.2 = (bf16[512,32,52]{0,2,1:T(8,128)(2,1)S(1)}, bf16[512,32,52]{0,2,1:T(8,128)(2,1)}, u32[]{:S(2)}) copy-start(bf16[512,32,52]{0,2,1:T(8,128)(2,1)} %reshape.131) | copy-start | bytes 5111812
  199.8 4.3 %copy-start.1 = (bf16[32,56,832]{2,1,0:T(8,128)(2,1)S(1)}, bf16[32,56,832]{2,1,0:T(8,128)(2,1)}, u32[]{:S(2)}) copy-start(bf16[32,56,832]{2,1,0:T(8,128)(2,1)} %get-tuple-element.12) | copy-start | bytes 8945668
  226.0 5.5 %copy-start = (bf16[32,56,832]{2,1,0:T(8,128)(2,1)S(1)}, bf16[32,56,832]{2,1,0:T(8,128)(2,1)}, u32[]{:S(2)}) copy-start(bf16[32,56,832]{2,1,0:T(8,128)(2,1)} %get-tuple-element.11) | copy-start | bytes 8945668
  241.0 2.0 slice-start
Sparse Core Ops, SparseCore 0:
  40.5 134.6 all-gather.5
  226.1 139.0 all-gather.3

commit v7 on v6

--- a/solution.py
+++ b/solution.py
@@ -1,7 +1,7 @@
 import jax
 import jax.numpy as jnp
 from jax import lax
-from jax.sharding import PartitionSpec as P
+from jax.sharding import Mesh, PartitionSpec as P
 
 HEAD_DIM = 104
 
@@ -59,18 +59,22 @@
 def local(tokens, attn_gain, qkv_weight, out_weight, merge_gain, merge_weight, segment_ids, owners):
     tok_rows = tokens.shape[0]
     n_dp = lax.axis_size("dp")
-    n_in = lax.axis_size("inner")
+    n_x = lax.axis_size("xx")
+    n_in = lax.axis_size("yl") * n_x
+    y_low = lax.axis_index("yl")
     lanes = n_in * qkv_weight.shape[-1]
     local_segment = lax.dynamic_slice_in_dim(
-        segment_ids, lax.axis_index("inner") * tok_rows, tok_rows
+        segment_ids, (y_low * n_x + lax.axis_index("xx")) * tok_rows, tok_rows
     )
     slabs = [pad_rows(qkv_weight[c]) for c in range(3)] + [pad_rows(out_weight.T)]
-    stacked = lax.all_gather(jnp.concatenate(slabs, axis=0), "inner", axis=1, tiled=True)
+    partner = lax.ppermute(merge_weight, "yl", [(0, 1), (1, 0)])
+    stacked = lax.all_gather(jnp.concatenate(slabs, axis=0), ("yl", "xx"), axis=1, tiled=True)
+    both = jnp.concatenate([merge_weight, partner], axis=1)
     real = qkv_weight.shape[1]
     tall = round8(real)
     stacked = stacked.reshape(4, tall, lanes)
-    merge_rows = -(-merge_weight.size // lanes)
-    flat = jnp.pad(merge_weight.reshape(-1), (0, merge_rows * lanes - merge_weight.size))
+    merge_rows = -(-both.size // lanes)
+    flat = jnp.pad(both.reshape(-1), (0, merge_rows * lanes - both.size))
     flat = flat.reshape(merge_rows, lanes)
     spare = min(4 * (tall - real), merge_rows)
     if spare:
@@ -90,7 +94,7 @@
         [gathered[:, :4, real:].reshape(n_dp, -1, lanes)[:, :spare], gathered[:, 4:].reshape(n_dp, -1, lanes)],
         axis=1,
     )
-    merge_full = merge_full.reshape(n_dp, -1)[:, : merge_weight.size].reshape(-1, merge_weight.shape[1])
+    merge_full = merge_full.reshape(n_dp, -1)[:, : both.size].reshape(-1, both.shape[1])
     normed = layer_norm(tokens, attn_gain).astype(jnp.bfloat16)
     normed = normed.reshape(tok_rows, n_dp, -1)
     normed = jnp.pad(normed, ((0, 0), (0, 0), (0, round8(normed.shape[-1]) - normed.shape[-1])))
@@ -116,11 +120,18 @@
     live = jnp.repeat(local_segment.reshape(-1, 4)[:, 0] >= 0, 4)
     merged = jnp.where(live[:, None], center * scale[:, None] * gain, 0.0).astype(jnp.bfloat16)
     merged = merged.reshape(tok_rows // 4, -1)
-    features = jnp.dot(
-        lax.all_gather(merged, "inner", axis=0, tiled=True),
+    mine = jnp.dot(
+        lax.all_gather(merged, "xx", axis=0, tiled=True),
         merge_full,
         preferred_element_type=jnp.float32,
     ).astype(jnp.bfloat16)
+    cols = merge_weight.shape[1]
+    swapped = lax.ppermute(mine[:, cols:], "yl", [(0, 1), (1, 0)])
+    features = jnp.where(
+        y_low == 0,
+        jnp.concatenate([mine[:, :cols], swapped], axis=0),
+        jnp.concatenate([swapped, mine[:, :cols]], axis=0),
+    )
     group_rows = features.shape[0]
     pick = (source_row[:, None] == jnp.arange(group_rows, dtype=jnp.int32)[None, :]).astype(jnp.bfloat16)
     outgoing = jnp.dot(pick, features, preferred_element_type=jnp.float32).astype(jnp.bfloat16)
@@ -128,16 +139,19 @@
 
 
 def solution(mesh):
+    dp, inner = "dp", ("yl", "xx")
+    n_dp, n_in = mesh.shape["dp"], mesh.shape["inner"]
+    split = Mesh(mesh.devices.reshape(n_dp, 2, n_in // 2), ("dp", "yl", "xx"))
     placed = (
-        P(("dp", "inner"), None),
+        P((dp, *inner), None),
         P(),
-        P(None, "dp", "inner"),
-        P("inner", "dp"),
+        P(None, dp, inner),
+        P(inner, dp),
         P(),
-        P("dp", "inner"),
-        P("dp"),
-        P("dp", None),
+        P(dp, inner),
+        P(dp),
+        P(dp, None),
     )
     return jax.shard_map(
-        local, mesh=mesh, in_specs=placed, out_specs=P("dp", "inner"), check_vma=False
+        local, mesh=split, in_specs=placed, out_specs=P(dp, inner), check_vma=False
     )

time: 428 us -> 378 us (0.88)
  waiting for transfers between devices: 222 us -> 175 us
    all_gather x1, waiting for transfers between devices: 119 us -> 44.4 us  [local(): lax.all_gather(merged, 'xx', axis=0, tiled=True)]
    all_gather x1, waiting for transfers between devices: 102 us -> 123 us  [local(): gathered = lax.all_gather(payload, 'dp', axis=0, tiled=False)]
    another operation x2 -> x3, local copies, waits for them, and re-layouts: 0.08 us -> 15.6 us  [the longest x1 15.5 us: local(): merge_full.reshape(n_dp, -1)[:, :both.size].reshape(-1, both.shape[1])]
    reshape x3 -> x0, local copies, waits for them, and re-layouts: 15.4 us -> none  [the longest x2 9.17 us: local(): merge_full.reshape(n_dp, -1)[:, :merge_weight.size]]
    dot_general x1, matrix products: 12.7 us -> 1.68 us  [local(): jnp.dot(pick, features, preferred_element_type=jnp.float32)]
    dot_general x0 -> x1, matrix products: none -> 8.54 us  [local(): jnp.dot(lax.all_gather(merged, 'xx', axis=0, tiled=True), merge_full, pre...]
    ppermute x0 -> x2, waiting for transfers between devices: none -> 7.05 us  [the longest x1 7.05 us: local(): swapped = lax.ppermute(mine[:, cols:], 'yl', [(0, 1), (1, 0)])]
    another operation x4, local copies, waits for them, and re-layouts: 12.1 us -> 7.73 us  [local(): gain = jnp.tile(merge_gain.reshape(4, -1), (tok_rows // 4, 1))]
  transfers between devices with their start and end apart: 2 -> 4, of which waited for: 2 -> 3; matrix products, arithmetic and copies ran while one was open for 12% -> 15% of each run, Pallas kernels for 0% -> 0%
where the time goes in v7:
time: 378 us; the launch traced here: 375 us
  waiting for transfers between devices  175 us (46%)
  blocking collectives  67.5 us (18%)
  local copies, waits for them, and re-layouts  56 us (15%)
  matrix products  35.6 us (9%)
  other arithmetic  25.9 us (7%)
  between operations  13.7 us (4%)
    all_gather x1, waiting for transfers between devices, local(): gathered = lax.all_gather(payload, 'dp', axis=0, tiled=False)  123 us
    all_gather x1, waiting for transfers between devices, local(): lax.all_gather(merged, 'xx', axis=0, tiled=True)  44.4 us
    all_to_all x1, blocking collectives, local(): lax.all_to_all(outgoing, 'dp', split_axis=0, concat_axis=0, tiled=True)  38.8 us
    all_gather x1, blocking collectives, local(): lax.all_gather(jnp.concatenate(slabs, axis=0), ('yl', 'xx'), axis=1, tile...  28.7 us
    another operation x1, local copies, waits for them, and re-layouts, local(): merge_full.reshape(n_dp, -1)[:, :both.size].reshape(-1, both.shape[1])  15.5 us
    dot_general x1, matrix products, local(): jnp.einsum('tgk,gckh->cth', normed, weights[:, :3], preferred_element_typ...  9.35 us
    another operation x3, other arithmetic  9.15 us
    dot_general x1, matrix products, local(): jnp.dot(lax.all_gather(merged, 'xx', axis=0, tiled=True), merge_full, pre...  8.54 us
  transfers between devices with their start and end apart: 4, of which 3 were waited for; matrix products, arithmetic and copies ran while one was open for 15% of the time, Pallas kernels for 0%

profile of v7, /device:TPU:30, one launch (start us, length us, event | category | flops | bytes accessed | tf_op | source)
XLA Modules:
  0.0 375.3 jit_solution(11143071988974656333)
XLA Ops:
  9.3 28.7 %all_gather.12 = bf16[224,832]{0,1:T(8,128)(2,1)S(1)} all-gather(bf16[224,104]{0,1:T(8,128)(2,1)S(1)} %fusion.41), channel_id=1, replica_groups=mesh['dp'=32,'yl'=2,'xx'=4] {'yl','xx'}, dimensions={1}, use_global_device_ids=true | all-gather | bytes 419328 | tf_op jit(solution)/shard_map/all_gather | solution.py:71
  42.2 2.4 tile.12
  44.7 4.9 %copy.56 = f32[512,1664]{0,1:T(8,128)} copy(f32[512,1664]{1,0:T(8,128)} %tile.12) | data formatting | bytes 6815744 | tf_op jit(solution)/shard_map/tile | solution.py:119
  49.5 0.9 broadcast_compare_fusion
  50.5 9.0 %reduce-window.6 = s32[32,8,128]{2,1,0:T(8,128)S(1)} reduce-window(s32[32,8,128]{2,1,0:T(8,128)S(1)} %fusion.32, s32[]{:T(128)} %constant.11.clone.1), window={size=1x1x128 pad=0_0x0_0x127_0}, to_apply=%region_0.1 | reduce-window | flops 4161536 | bytes 262148 | tf_op jit(solution)/shard_map/reduce-window
  60.0 4.5 %scatter_custom_fusion = s32[2048]{0:T(1024)S(1)} fusion(s32[1024]{0:T(1024)S(1)} %bitcast.93, s32[1024]{0:T(1024)S(1)} %iota.15, s32[]{:T(128)} %constant.18.clone.1), kind=kCustom, calls=%fused_computation.73 | custom fusion | bytes 8196 | tf_op jit(solution)/shard_map/scatter | solution.py:55
  64.5 1.4 copy.52
  67.3 1.4 reshape.126
  68.7 123.4 %all-gather.6.cloned.1.call-done = bf16[192,56,832]{2,1,0:T(8,128)(2,1)} async-done(((bf16[6,56,832]{2,1,0:T(8,128)(2,1)}), bf16[192,56,832]{2,1,0:T(8,128)(2,1)}) %all-gather.6.cloned.1.call-update) | async-done | bytes 17891344 | tf_op jit(solution)/shard_map/all_gather | solution.py:88
  192.1 3.8 %slice_bitcast_fusion = bf16[32,56,832]{2,1,0:T(8,128)(2,1)} fusion(bf16[32,6,56,832]{3,2,1,0:T(8,128)(2,1)} %bitcast.73), kind=kLoop, calls=%fused_computation.27 | loop fusion | bytes 5963776 | tf_op jit(solution)/shard_map/squeeze | solution.py:110
  195.9 9.3 %fusion.16 = bf16[3,512,832]{1,2,0:T(8,128)(2,1)S(1)} fusion(bf16[32,6,56,832]{3,2,1,0:T(8,128)(2,1)} %bitcast.74, bf16[512,32,52]{0,2,1:T(8,128)(2,1)S(1)} %copy-done.1), kind=kOutput, calls=%fused_computation.29 | convolution fusion | flops 4581457920 | bytes 22151168 | tf_op jit(solution)/shard_map/tgk,gckh->cth/dot_general | solution.py:101
  205.3 1.1 fusion.49
  206.4 7.8 %fusion.52 = (f32[8,512]{1,0:T(8,128)S(1)}, f32[8,512,512]{1,2,0:T(8,128)}) fusion(pred[512,512]{0,1:T(8,128)(4,1)} %broadcast_compare_fusion, bf16[512,8,104]{0,2,1:T(8,128)(2,1)} %bitcast.83, bf16[512,8,104]{0,2,1:T(8,128)(2,1)S(1)} %bitcast.82), kind=kOutput, calls=%fused_computation.86 | convolution fusion | flops 444596736 | bytes 10371072 | tf_op jit(solution)/shard_map/sub | solution.py:26
  214.2 4.3 %fusion.19 = bf16[8,104,512]{2,1,0:T(8,128)(2,1)S(1)} fusion(bf16[512,8,104]{0,2,1:T(8,128)(2,1)S(1)} %bitcast.81, f32[8,512,512]{1,2,0:T(8,128)} %get-tuple-element.20, f32[8,512]{1,0:T(8,128)S(1)} %get-tuple-element.19), kind=kOutput, calls=%fused_computation.32 | convolution fusion | flops 440827904 | bytes 10108928 | tf_op jit(solution)/shard_map/hqk,khe->qhe/dot_general | solution.py:28
  218.5 3.9 %fusion.13 = f32[512,32,52]{0,2,1:T(8,128)} fusion(bf16[512,832,1]{0,1,2:T(8,128)(2,1)S(1)} %bitcast.94, bf16[32,56,832]{2,1,0:T(8,128)(2,1)S(1)} %copy-done), kind=kOutput, calls=%fused_computation.25 | convolution fusion | flops 1417674752 | bytes 7241728 | tf_op jit(solution)/shard_map/tf,gkf->tgk/dot_general | solution.py:109
  222.5 4.7 %reshape.128 = f32[512,1664]{0,1:T(8,128)} reshape(f32[512,32,52]{0,2,1:T(8,128)} %fusion.13) | data formatting | bytes 6815744 | tf_op jit(solution)/shard_map/reshape | solution.py:112
  227.2 2.4 fusion.20
  230.0 2.6 multiply_reduce_fusion
  233.0 4.0 %select_convert_fusion = bf16[512,1664]{0,1:T(8,128)(2,1)S(1)} fusion(f32[512,1664]{0,1:T(8,128)} %copy.56, f32[512]{0:T(512)S(1)} %mul.70, f32[512]{0:T(512)S(1)} %sub.34, pred[512]{0:T(512)(128)(4,1)S(1)} %broadcast_in_dim.52, f32[512,1664]{0,1:T(8,128)} %reshape.128, bf16[512,1664]{0,1:T(8,128)(2,1)S(1)} %copy.52), kind=kLoop, calls=%fused_computation.23 | loop fusion | flops 5963776 | bytes 10228224 | tf_op jit(solution)/shard_map/convert_element_type | solution.py:121
  237.1 1.4 copy.57
  238.5 2.1 reshape.131
  240.6 3.3 slice.98
  244.0 2.0 slice.97
  246.4 4.1 %pad_maximum_fusion = bf16[32,128,832]{2,1,0:T(8,128)(2,1)} fusion(bf16[32,112,832]{2,1,0:T(8,128)(2,1)S(1)} %bitcast.72, bf16[32,16,832]{2,1,0:T(8,128)(2,1)S(1)} %copy.59), kind=kLoop, calls=%fused_computation.7 | loop fusion | flops 13631488 | bytes 13631488 | tf_op jit(solution)/shard_map/concatenate | solution.py:93
  250.5 15.5 %reshape_reshape.3 = bf16[6656,512]{1,0:T(8,128)(2,1)} reshape(bf16[32,128,832]{2,1,0:T(8,128)(2,1)} %pad_maximum_fusion) | data formatting | bytes 13631488 | tf_op jit(solution)/shard_map/reshape;reshape | solution.py:97
  266.0 44.4 %all-gather.4.cloned.1.call-done = bf16[512,6656]{1,0:T(8,128)(2,1)} async-done(((bf16[128,6656]{1,0:T(8,128)(2,1)}), bf16[512,6656]{1,0:T(8,128)(2,1)}) %all-gather.4.cloned.1.call-update) | async-done | bytes 6815760 | tf_op jit(solution)/shard_map/all_gather | solution.py:124
  310.4 8.5 %convolution_convert_fusion = bf16[512,512]{1,0:T(8,128)(2,1)S(1)} fusion(bf16[512,6656]{1,0:T(8,128)(2,1)} %all-gather.4.cloned.1.call-done, bf16[6656,512]{1,0:T(8,128)(2,1)} %reshape_reshape.3), kind=kOutput, calls=%fused_computation.33 | convolution fusion | flops 3489923072 | bytes 14155776 | tf_op jit(solution)/shard_map/dot_general | solution.py:123
  319.0 0.9 collective-permute-start.1
  319.9 7.0 %collective-permute-done.1 = bf16[512,256]{1,0:T(8,128)(2,1)S(1)} collective-permute-done((bf16[512,256]{1,0:T(8,128)(2,1)S(1)}, bf16[512,256]{1,0:T(8,128)(2,1)S(1)}, u32[]{:S(2)}, u32[]{:S(2)}) %collective-permute-start.1) | collective-permute-done | bytes 262176 | tf_op jit(solution)/shard_map/ppermute | solution.py:129
  327.0 1.7 fusion.15
  328.6 38.8 %all_to_all.12 = bf16[32,64,256]{2,1,0:T(8,128)(2,1)S(1)} all-to-all(bf16[32,64,256]{2,1,0:T(8,128)(2,1)S(1)} %bitcast.80), channel_id=1, replica_groups=mesh['dp'=32,'yl'=2,'xx'=4] {'dp'}, dimensions={0} | all-to-all | bytes 2097152 | tf_op jit(solution)/shard_map/all_to_all | solution.py:138
  367.5 1.0 copy.71
  (67 shorter events, 10.1 us)
Async XLA Ops:
  6.5 35.2 %copy-start.4 = (f32[6656]{0:T(1024)S(1)}, f32[6656]{0:T(1024)}, u32[]{:S(2)}) copy-start(f32[6656]{0:T(1024)} %param.12) | copy-start | bytes 79876
  6.5 185.6 %all-gather.6.cloned.1.call-start = ((), (), s32[]{:S(2)}) async-start(), calls=%async_computation.2 | async-start | bytes 19869696 | tf_op jit(solution)/shard_map/all_gather | solution.py:88
  6.5 32.6 %collective-permute-start = (bf16[208,256]{1,0:T(8,128)(2,1)}, bf16[208,256]{1,0:T(8,128)(2,1)S(1)}, u32[]{:S(2)}, u32[]{:S(2)}) collective-permute-start(bf16[208,256]{1,0:T(8,128)(2,1)} %param.13), channel_id=1, source_target_pairs={{0,4},{4,0},{1,5},{5,1},{2,6},{6,2},{3,7},{7,3},{8,12},{12,8},{9,1... | collective-permute-start | bytes 319496 | tf_op jit(solution)/shard_map/ppermute | solution.py:70
  40.5 269.9 %all-gather.4.cloned.1.call-start = ((), (), s32[]{:S(2)}) async-start(), calls=%async_computation.1 | async-start | bytes 8519680 | tf_op jit(solution)/shard_map/all_gather | solution.py:124
  44.6 5.8 %copy-start.3 = (s32[1024,1]{0,1:T(1,128)S(1)}, s32[1024,1]{0,1:T(1,128)}, u32[]{:S(2)}) copy-start(s32[1024,1]{0,1:T(1,128)} %param.15) | copy-start | bytes 12292
  44.7 19.9 %copy-start.2 = (bf16[512,1664]{1,0:T(8,128)(2,1)S(1)}, bf16[512,1664]{1,0:T(8,128)(2,1)}, u32[]{:S(2)}) copy-start(bf16[512,1664]{1,0:T(8,128)(2,1)} %param.8) | copy-start | bytes 5111812
  64.5 2.2 copy-start.5
  68.7 127.2 %copy-start.1 = (bf16[512,32,52]{0,2,1:T(8,128)(2,1)S(1)}, bf16[512,32,52]{0,2,1:T(8,128)(2,1)}, u32[]{:S(2)}) copy-start(bf16[512,32,52]{0,2,1:T(8,128)(2,1)} %reshape.126) | copy-start | bytes 5111812
  214.2 4.3 %copy-start = (bf16[32,56,832]{2,1,0:T(8,128)(2,1)S(1)}, bf16[32,56,832]{2,1,0:T(8,128)(2,1)}, u32[]{:S(2)}) copy-start(bf16[32,56,832]{2,1,0:T(8,128)(2,1)} %slice_bitcast_fusion) | copy-start | bytes 8945668
  319.0 8.0 %collective-permute-start.1 = (bf16[512,256]{1,0:T(8,128)(2,1)S(1)}, bf16[512,256]{1,0:T(8,128)(2,1)S(1)}, u32[]{:S(2)}, u32[]{:S(2)}) collective-permute-start(bf16[512,256]{1,0:T(8,128)(2,1)S(1)} %get-tuple-element.15), channel_id=1, source_target_pairs={{0,4},{4,0},{1,5},{5,1},{2,6},{6,2},{3,7},{7,3},{8,12},{12,8},{9,1... | collective-permute-start | bytes 786440 | tf_op jit(solution)/shard_map/ppermute | solution.py:129
Sparse Core Ops, SparseCore 0:
  40.6 151.4 all-gather.5
  240.7 69.6 all-gather.3

commit v8 on v7

--- a/solution.py
+++ b/solution.py
@@ -120,17 +120,16 @@
     live = jnp.repeat(local_segment.reshape(-1, 4)[:, 0] >= 0, 4)
     merged = jnp.where(live[:, None], center * scale[:, None] * gain, 0.0).astype(jnp.bfloat16)
     merged = merged.reshape(tok_rows // 4, -1)
-    mine = jnp.dot(
-        lax.all_gather(merged, "xx", axis=0, tiled=True),
-        merge_full,
-        preferred_element_type=jnp.float32,
-    ).astype(jnp.bfloat16)
+    rows_x = lax.all_gather(merged, "xx", axis=0, tiled=True)
     cols = merge_weight.shape[1]
-    swapped = lax.ppermute(mine[:, cols:], "yl", [(0, 1), (1, 0)])
+    theirs = jnp.dot(rows_x, merge_full[:, cols:], preferred_element_type=jnp.float32)
+    swapped = lax.ppermute(theirs.astype(jnp.bfloat16), "yl", [(0, 1), (1, 0)])
+    own = jnp.dot(rows_x, merge_full[:, :cols], preferred_element_type=jnp.float32)
+    own, swapped = lax.optimization_barrier((own.astype(jnp.bfloat16), swapped))
     features = jnp.where(
         y_low == 0,
-        jnp.concatenate([mine[:, :cols], swapped], axis=0),
-        jnp.concatenate([swapped, mine[:, :cols]], axis=0),
+        jnp.concatenate([own, swapped], axis=0),
+        jnp.concatenate([swapped, own], axis=0),
     )
     group_rows = features.shape[0]
     pick = (source_row[:, None] == jnp.arange(group_rows, dtype=jnp.int32)[None, :]).astype(jnp.bfloat16)

time: 378 us -> 376 us (level)
    dot_general x1 -> x2, matrix products: 8.54 us -> 7.88 us  [the longest x1 5.97 us: local(): jnp.dot(rows_x, merge_full[:, cols:], preferred_element_type=jnp.float32)]
  transfers between devices with their start and end apart: 4 -> 4, of which waited for: 3 -> 3; matrix products, arithmetic and copies ran while one was open for 15% -> 16% of each run, Pallas kernels for 0% -> 0%
where the time goes in v8:
time: 376 us; the launch traced here: 373 us
  waiting for transfers between devices  172 us (46%)
  blocking collectives  67.5 us (18%)
  local copies, waits for them, and re-layouts  56.6 us (15%)
  matrix products  35 us (9%)
  other arithmetic  25.9 us (7%)
  between operations  13.7 us (4%)
    all_gather x1, waiting for transfers between devices, local(): gathered = lax.all_gather(payload, 'dp', axis=0, tiled=False)  123 us
    all_gather x1, waiting for transfers between devices, local(): rows_x = lax.all_gather(merged, 'xx', axis=0, tiled=True)  44.4 us
    all_to_all x1, blocking collectives, local(): lax.all_to_all(outgoing, 'dp', split_axis=0, concat_axis=0, tiled=True)  38.8 us
    all_gather x1, blocking collectives, local(): lax.all_gather(jnp.concatenate(slabs, axis=0), ('yl', 'xx'), axis=1, tile...  28.7 us
    another operation x1, local copies, waits for them, and re-layouts, local(): merge_full.reshape(n_dp, -1)[:, :both.size].reshape(-1, both.shape[1])  15.5 us
    dot_general x1, matrix products, local(): jnp.einsum('tgk,gckh->cth', normed, weights[:, :3], preferred_element_typ...  9.35 us
    another operation x3, other arithmetic  9.15 us
    sub x1, matrix products, attend_block(): weights = jnp.exp(scores - top)  7.82 us
  transfers between devices with their start and end apart: 4, of which 3 were waited for; matrix products, arithmetic and copies ran while one was open for 16% of the time, Pallas kernels for 0%

profile of v8, /device:TPU:30, one launch (start us, length us, event | category | flops | bytes accessed | tf_op | source)
XLA Modules:
  0.0 372.9 jit_solution(12562984187349248261)
XLA Ops:
  9.3 28.7 %all_gather.12 = bf16[224,832]{0,1:T(8,128)(2,1)S(1)} all-gather(bf16[224,104]{0,1:T(8,128)(2,1)S(1)} %fusion.51), channel_id=1, replica_groups=mesh['dp'=32,'yl'=2,'xx'=4] {'yl','xx'}, dimensions={1}, use_global_device_ids=true | all-gather | bytes 419328 | tf_op jit(solution)/shard_map/all_gather | solution.py:71
  42.2 2.4 tile.12
  44.7 4.9 %copy.56 = f32[512,1664]{0,1:T(8,128)} copy(f32[512,1664]{1,0:T(8,128)} %tile.12) | data formatting | bytes 6815744 | tf_op jit(solution)/shard_map/tile | solution.py:119
  50.5 9.0 %reduce-window.6 = s32[32,8,128]{2,1,0:T(8,128)S(1)} reduce-window(s32[32,8,128]{2,1,0:T(8,128)S(1)} %fusion.42, s32[]{:T(128)} %constant.11.clone.1), window={size=1x1x128 pad=0_0x0_0x127_0}, to_apply=%region_0.1 | reduce-window | flops 4161536 | bytes 262148 | tf_op jit(solution)/shard_map/reduce-window
  60.0 4.5 %scatter_custom_fusion = s32[2048]{0:T(1024)S(1)} fusion(s32[1024]{0:T(1024)S(1)} %bitcast.93, s32[1024]{0:T(1024)S(1)} %iota.15, s32[]{:T(128)} %constant.18.clone.1), kind=kCustom, calls=%fused_computation.78 | custom fusion | bytes 8196 | tf_op jit(solution)/shard_map/scatter | solution.py:55
  64.5 1.4 copy.52
  67.3 1.4 reshape.126
  68.7 123.4 %all-gather.6.cloned.1.call-done = bf16[192,56,832]{2,1,0:T(8,128)(2,1)} async-done(((bf16[6,56,832]{2,1,0:T(8,128)(2,1)}), bf16[192,56,832]{2,1,0:T(8,128)(2,1)}) %all-gather.6.cloned.1.call-update) | async-done | bytes 17891344 | tf_op jit(solution)/shard_map/all_gather | solution.py:88
  192.1 3.8 %slice_bitcast_fusion = bf16[32,56,832]{2,1,0:T(8,128)(2,1)} fusion(bf16[32,6,56,832]{3,2,1,0:T(8,128)(2,1)} %bitcast.73), kind=kLoop, calls=%fused_computation.31 | loop fusion | bytes 5963776 | tf_op jit(solution)/shard_map/squeeze | solution.py:110
  195.9 9.3 %fusion.20 = bf16[3,512,832]{1,2,0:T(8,128)(2,1)S(1)} fusion(bf16[32,6,56,832]{3,2,1,0:T(8,128)(2,1)} %bitcast.74, bf16[512,32,52]{0,2,1:T(8,128)(2,1)S(1)} %copy-done.2), kind=kOutput, calls=%fused_computation.33 | convolution fusion | flops 4581457920 | bytes 22151168 | tf_op jit(solution)/shard_map/tgk,gckh->cth/dot_general | solution.py:101
  205.3 1.1 fusion.59
  206.4 7.8 %fusion.61 = (f32[8,512]{1,0:T(8,128)S(1)}, f32[8,512,512]{1,2,0:T(8,128)}) fusion(pred[512,512]{0,1:T(8,128)(4,1)} %broadcast_compare_fusion, bf16[512,8,104]{0,2,1:T(8,128)(2,1)} %bitcast.83, bf16[512,8,104]{0,2,1:T(8,128)(2,1)S(1)} %bitcast.82), kind=kOutput, calls=%fused_computation.90 | convolution fusion | flops 444596736 | bytes 10371072 | tf_op jit(solution)/shard_map/sub | solution.py:26
  214.2 4.3 %fusion.23 = bf16[8,104,512]{2,1,0:T(8,128)(2,1)S(1)} fusion(bf16[512,8,104]{0,2,1:T(8,128)(2,1)S(1)} %bitcast.81, f32[8,512,512]{1,2,0:T(8,128)} %get-tuple-element.22, f32[8,512]{1,0:T(8,128)S(1)} %get-tuple-element.21), kind=kOutput, calls=%fused_computation.36 | convolution fusion | flops 440827904 | bytes 10108928 | tf_op jit(solution)/shard_map/hqk,khe->qhe/dot_general | solution.py:28
  218.5 3.9 %fusion.17 = f32[512,32,52]{0,2,1:T(8,128)} fusion(bf16[512,832,1]{0,1,2:T(8,128)(2,1)S(1)} %bitcast.94, bf16[32,56,832]{2,1,0:T(8,128)(2,1)S(1)} %copy-done.1), kind=kOutput, calls=%fused_computation.29 | convolution fusion | flops 1417674752 | bytes 7241728 | tf_op jit(solution)/shard_map/tf,gkf->tgk/dot_general | solution.py:109
  222.5 4.7 %reshape.128 = f32[512,1664]{0,1:T(8,128)} reshape(f32[512,32,52]{0,2,1:T(8,128)} %fusion.17) | data formatting | bytes 6815744 | tf_op jit(solution)/shard_map/reshape | solution.py:112
  227.2 2.4 fusion.24
  230.0 2.6 multiply_reduce_fusion
  233.0 4.0 %select_convert_fusion = bf16[512,1664]{0,1:T(8,128)(2,1)S(1)} fusion(f32[512,1664]{0,1:T(8,128)} %copy.56, f32[512]{0:T(512)S(1)} %mul.70, f32[512]{0:T(512)S(1)} %sub.34, pred[512]{0:T(512)(128)(4,1)S(1)} %broadcast_in_dim.52, f32[512,1664]{0,1:T(8,128)} %reshape.128, bf16[512,1664]{0,1:T(8,128)(2,1)S(1)} %copy.52), kind=kLoop, calls=%fused_computation.27 | loop fusion | flops 5963776 | bytes 10228224 | tf_op jit(solution)/shard_map/convert_element_type | solution.py:121
  237.1 1.4 copy.57
  238.5 2.1 reshape.131
  240.6 3.3 slice.97
  244.0 2.0 slice.96
  246.4 4.1 %pad_maximum_fusion = bf16[32,128,832]{2,1,0:T(8,128)(2,1)} fusion(bf16[32,112,832]{2,1,0:T(8,128)(2,1)S(1)} %bitcast.72, bf16[32,16,832]{2,1,0:T(8,128)(2,1)S(1)} %copy.59), kind=kLoop, calls=%fused_computation.7 | loop fusion | flops 13631488 | bytes 13631488 | tf_op jit(solution)/shard_map/concatenate | solution.py:93
  250.5 15.5 %reshape_reshape.3 = bf16[6656,512]{1,0:T(8,128)(2,1)} reshape(bf16[32,128,832]{2,1,0:T(8,128)(2,1)} %pad_maximum_fusion) | data formatting | bytes 13631488 | tf_op jit(solution)/shard_map/reshape;reshape | solution.py:97
  266.0 44.4 %all-gather.4.cloned.1.call-done = bf16[512,6656]{1,0:T(8,128)(2,1)} async-done(((bf16[128,6656]{1,0:T(8,128)(2,1)}), bf16[512,6656]{1,0:T(8,128)(2,1)}) %all-gather.4.cloned.1.call-update) | async-done | bytes 6815760 | tf_op jit(solution)/shard_map/all_gather | solution.py:123
  310.4 6.0 %fusion.28 = bf16[512,256]{1,0:T(8,128)(2,1)S(1)} fusion(bf16[512,6656]{1,0:T(8,128)(2,1)} %all-gather.4.cloned.1.call-done, bf16[6656,512]{1,0:T(8,128)(2,1)} %reshape_reshape.3), kind=kOutput, calls=%fused_computation.39 | convolution fusion | flops 1744961536 | bytes 10485760 | tf_op jit(solution)/shard_map/dot_general | solution.py:125
  316.4 1.2 collective-permute-start.1
  318.2 1.9 fusion.25
  320.1 4.5 %collective-permute-done.1 = bf16[512,256]{1,0:T(8,128)(2,1)S(1)} collective-permute-done((bf16[512,256]{1,0:T(8,128)(2,1)S(1)}, bf16[512,256]{1,0:T(8,128)(2,1)S(1)}, u32[]{:S(2)}, u32[]{:S(2)}) %collective-permute-start.1) | collective-permute-done | bytes 262176 | tf_op jit(solution)/shard_map/ppermute | solution.py:126
  324.6 1.7 fusion.19
  326.3 38.8 %all_to_all.12 = bf16[32,64,256]{2,1,0:T(8,128)(2,1)S(1)} all-to-all(bf16[32,64,256]{2,1,0:T(8,128)(2,1)S(1)} %bitcast.80), channel_id=1, replica_groups=mesh['dp'=32,'yl'=2,'xx'=4] {'dp'}, dimensions={0} | all-to-all | bytes 2097152 | tf_op jit(solution)/shard_map/all_to_all | solution.py:137
  365.1 1.0 copy.71
  (71 shorter events, 11.6 us)
Async XLA Ops:
  6.5 35.2 %copy-start.5 = (f32[6656]{0:T(1024)S(1)}, f32[6656]{0:T(1024)}, u32[]{:S(2)}) copy-start(f32[6656]{0:T(1024)} %param.12) | copy-start | bytes 79876
  6.5 185.6 %all-gather.6.cloned.1.call-start = ((), (), s32[]{:S(2)}) async-start(), calls=%async_computation.2 | async-start | bytes 19869696 | tf_op jit(solution)/shard_map/all_gather | solution.py:88
  6.5 32.6 %collective-permute-start = (bf16[208,256]{1,0:T(8,128)(2,1)}, bf16[208,256]{1,0:T(8,128)(2,1)S(1)}, u32[]{:S(2)}, u32[]{:S(2)}) collective-permute-start(bf16[208,256]{1,0:T(8,128)(2,1)} %param.13), channel_id=1, source_target_pairs={{0,4},{4,0},{1,5},{5,1},{2,6},{6,2},{3,7},{7,3},{8,12},{12,8},{9,1... | collective-permute-start | bytes 319496 | tf_op jit(solution)/shard_map/ppermute | solution.py:70
  40.5 269.9 %all-gather.4.cloned.1.call-start = ((), (), s32[]{:S(2)}) async-start(), calls=%async_computation.1 | async-start | bytes 8519680 | tf_op jit(solution)/shard_map/all_gather | solution.py:123
  44.6 5.8 %copy-start.4 = (s32[1024,1]{0,1:T(1,128)S(1)}, s32[1024,1]{0,1:T(1,128)}, u32[]{:S(2)}) copy-start(s32[1024,1]{0,1:T(1,128)} %param.15) | copy-start | bytes 12292
  44.7 19.9 %copy-start.3 = (bf16[512,1664]{1,0:T(8,128)(2,1)S(1)}, bf16[512,1664]{1,0:T(8,128)(2,1)}, u32[]{:S(2)}) copy-start(bf16[512,1664]{1,0:T(8,128)(2,1)} %param.8) | copy-start | bytes 5111812
  64.5 2.2 copy-start.6
  68.7 127.2 %copy-start.2 = (bf16[512,32,52]{0,2,1:T(8,128)(2,1)S(1)}, bf16[512,32,52]{0,2,1:T(8,128)(2,1)}, u32[]{:S(2)}) copy-start(bf16[512,32,52]{0,2,1:T(8,128)(2,1)} %reshape.126) | copy-start | bytes 5111812
  214.2 4.3 %copy-start.1 = (bf16[32,56,832]{2,1,0:T(8,128)(2,1)S(1)}, bf16[32,56,832]{2,1,0:T(8,128)(2,1)}, u32[]{:S(2)}) copy-start(bf16[32,56,832]{2,1,0:T(8,128)(2,1)} %slice_bitcast_fusion) | copy-start | bytes 8945668
  310.4 7.2 %copy-start = (bf16[6656,512]{1,0:T(8,128)(2,1)S(1)}, bf16[6656,512]{1,0:T(8,128)(2,1)}, u32[]{:S(2)}) copy-start(bf16[6656,512]{1,0:T(8,128)(2,1)} %reshape_reshape.3) | copy-start | bytes 20447236
  310.4 7.8 %copy-start.7 = (bf16[512,6656]{1,0:T(8,128)(2,1)S(1)}, bf16[512,6656]{1,0:T(8,128)(2,1)}, u32[]{:S(2)}) copy-start(bf16[512,6656]{1,0:T(8,128)(2,1)} %all-gather.4.cloned.1.call-done) | copy-start | bytes 20447236
  316.4 8.2 %collective-permute-start.1 = (bf16[512,256]{1,0:T(8,128)(2,1)S(1)}, bf16[512,256]{1,0:T(8,128)(2,1)S(1)}, u32[]{:S(2)}, u32[]{:S(2)}) collective-permute-start(bf16[512,256]{1,0:T(8,128)(2,1)S(1)} %fusion.28), channel_id=1, source_target_pairs={{0,4},{4,0},{1,5},{5,1},{2,6},{6,2},{3,7},{7,3},{8,12},{12,8},{9,1... | collective-permute-start | bytes 786440 | tf_op jit(solution)/shard_map/ppermute | solution.py:126
Sparse Core Ops, SparseCore 0:
  40.6 151.4 all-gather.5
  240.7 69.6 all-gather.3

commit v9 on v8

--- a/solution.py
+++ b/solution.py
@@ -67,16 +67,15 @@
         segment_ids, (y_low * n_x + lax.axis_index("xx")) * tok_rows, tok_rows
     )
     slabs = [pad_rows(qkv_weight[c]) for c in range(3)] + [pad_rows(out_weight.T)]
-    partner = lax.ppermute(merge_weight, "yl", [(0, 1), (1, 0)])
     stacked = lax.all_gather(jnp.concatenate(slabs, axis=0), ("yl", "xx"), axis=1, tiled=True)
-    both = jnp.concatenate([merge_weight, partner], axis=1)
+    both = merge_weight
     real = qkv_weight.shape[1]
     tall = round8(real)
     stacked = stacked.reshape(4, tall, lanes)
     merge_rows = -(-both.size // lanes)
     flat = jnp.pad(both.reshape(-1), (0, merge_rows * lanes - both.size))
     flat = flat.reshape(merge_rows, lanes)
-    spare = min(4 * (tall - real), merge_rows)
+    spare = min(4 * (tall - real), merge_rows // 4 * 4)
     if spare:
         tail = flat[:spare].reshape(4, spare // 4, lanes)
         tail = jnp.pad(tail, ((0, 0), (0, tall - real - spare // 4), (0, 0)))
@@ -91,7 +90,10 @@
     source_row, tokens = lax.optimization_barrier((source_row, tokens))
     weights = gathered[:, :4]
     merge_full = jnp.concatenate(
-        [gathered[:, :4, real:].reshape(n_dp, -1, lanes)[:, :spare], gathered[:, 4:].reshape(n_dp, -1, lanes)],
+        [
+            gathered[:, :4, real : real + spare // 4].reshape(n_dp, -1, lanes),
+            gathered[:, 4:].reshape(n_dp, -1, lanes),
+        ],
         axis=1,
     )
     merge_full = merge_full.reshape(n_dp, -1)[:, : both.size].reshape(-1, both.shape[1])
@@ -122,9 +124,10 @@
     merged = merged.reshape(tok_rows // 4, -1)
     rows_x = lax.all_gather(merged, "xx", axis=0, tiled=True)
     cols = merge_weight.shape[1]
-    theirs = jnp.dot(rows_x, merge_full[:, cols:], preferred_element_type=jnp.float32)
+    partner = lax.ppermute(merge_full, "yl", [(0, 1), (1, 0)])
+    theirs = jnp.dot(rows_x, partner, preferred_element_type=jnp.float32)
     swapped = lax.ppermute(theirs.astype(jnp.bfloat16), "yl", [(0, 1), (1, 0)])
-    own = jnp.dot(rows_x, merge_full[:, :cols], preferred_element_type=jnp.float32)
+    own = jnp.dot(rows_x, merge_full, preferred_element_type=jnp.float32)
     own, swapped = lax.optimization_barrier((own.astype(jnp.bfloat16), swapped))
     features = jnp.where(
         y_low == 0,

time: 376 us -> 383 us (1.019)
  waiting for transfers between devices: 172 us -> 184 us
    ppermute x1, waiting for transfers between devices: 0.01 us -> 76.1 us  [local(): partner = lax.ppermute(merge_full, 'yl', [(0, 1), (1, 0)])]
    all_gather x1, waiting for transfers between devices: 44.4 us -> 0.01 us  [local(): rows_x = lax.all_gather(merged, 'xx', axis=0, tiled=True)]
    all_gather x1, waiting for transfers between devices: 123 us -> 102 us  [local(): gathered = lax.all_gather(payload, 'dp', axis=0, tiled=False)]
    reshape x1 -> x4, local copies, waits for them, and re-layouts: 0.28 us -> 17.9 us  [the longest x2 9.35 us: local(): merge_full.reshape(n_dp, -1)[:, :both.size].reshape(-1, both.shape[1])]
    another operation x3 -> x2, local copies, waits for them, and re-layouts: 15.6 us -> 0.08 us  [the longest x1 15.5 us: local(): merge_full.reshape(n_dp, -1)[:, :both.size].reshape(-1, both.shape[1])]
    another operation x4, local copies, waits for them, and re-layouts: 7.73 us -> 12.1 us  [local(): gain = jnp.tile(merge_gain.reshape(4, -1), (tok_rows // 4, 1))]
    squeeze x1 -> x0, local copies, waits for them, and re-layouts: 3.83 us -> none  [local(): weights[:, 3]]
  transfers between devices with their start and end apart: 4 -> 4, of which waited for: 3 -> 3; matrix products, arithmetic and copies ran while one was open for 16% -> 14% of each run, Pallas kernels for 0% -> 0%
where the time goes in v9:
time: 383 us; the launch traced here: 382 us
  waiting for transfers between devices  184 us (48%)
  blocking collectives  65 us (17%)
  local copies, waits for them, and re-layouts  58.6 us (15%)
  matrix products  34.9 us (9%)
  other arithmetic  25.2 us (7%)
  between operations  13.7 us (4%)
    all_gather x1, waiting for transfers between devices, local(): gathered = lax.all_gather(payload, 'dp', axis=0, tiled=False)  102 us
    ppermute x1, waiting for transfers between devices, local(): partner = lax.ppermute(merge_full, 'yl', [(0, 1), (1, 0)])  76.1 us
    all_to_all x1, blocking collectives, local(): lax.all_to_all(outgoing, 'dp', split_axis=0, concat_axis=0, tiled=True)  36.3 us
    all_gather x1, blocking collectives, local(): lax.all_gather(jnp.concatenate(slabs, axis=0), ('yl', 'xx'), axis=1, tile...  28.7 us
    another operation x4, local copies, waits for them, and re-layouts, local(): gain = jnp.tile(merge_gain.reshape(4, -1), (tok_rows // 4, 1))  12.1 us
    dot_general x1, matrix products, local(): jnp.einsum('tgk,gckh->cth', normed, weights[:, :3], preferred_element_typ...  9.52 us
    reshape x2, local copies, waits for them, and re-layouts, local(): merge_full.reshape(n_dp, -1)[:, :both.size].reshape(-1, both.shape[1])  9.35 us
    another operation x3, other arithmetic  9.15 us
  transfers between devices with their start and end apart: 4, of which 3 were waited for; matrix products, arithmetic and copies ran while one was open for 14% of the time, Pallas kernels for 0%

profile of v9, /device:TPU:30, one launch (start us, length us, event | category | flops | bytes accessed | tf_op | source)
XLA Modules:
  0.0 381.9 jit_solution(17344156148311674445)
XLA Ops:
  10.6 28.7 %all_gather.12 = bf16[224,832]{0,1:T(8,128)(2,1)S(1)} all-gather(bf16[224,104]{0,1:T(8,128)(2,1)S(1)} %fusion.41), channel_id=1, replica_groups=mesh['dp'=32,'yl'=2,'xx'=4] {'yl','xx'}, dimensions={1}, use_global_device_ids=true | all-gather | bytes 419328 | tf_op jit(solution)/shard_map/all_gather | solution.py:70
  41.7 9.0 %reduce-window.6 = s32[32,8,128]{2,1,0:T(8,128)S(1)} reduce-window(s32[32,8,128]{2,1,0:T(8,128)S(1)} %fusion.32, s32[]{:T(128)} %constant.11.clone.1), window={size=1x1x128 pad=0_0x0_0x127_0}, to_apply=%region_0.1 | reduce-window | flops 4161536 | bytes 262148 | tf_op jit(solution)/shard_map/reduce-window
  51.3 4.3 %scatter_custom_fusion = s32[2048]{0:T(1024)S(1)} fusion(s32[1024]{0:T(1024)S(1)} %bitcast.95, s32[1024]{0:T(1024)S(1)} %iota.15, s32[]{:T(128)} %constant.18.clone.1), kind=kCustom, calls=%fused_computation.74 | custom fusion | bytes 8196 | tf_op jit(solution)/shard_map/scatter | solution.py:55
  55.6 1.4 copy.47
  58.4 1.4 reshape.131
  59.8 2.2 tile.11
  62.0 5.1 %tile.12 = f32[512,1664]{1,0:T(8,128)} reshape(f32[128,4,1664]{2,1,0:T(4,128)} %tile.11) | data formatting | bytes 6815744 | tf_op jit(solution)/shard_map/tile | solution.py:121
  67.1 4.8 %copy.51 = f32[512,1664]{0,1:T(8,128)} copy(f32[512,1664]{1,0:T(8,128)} %tile.12) | data formatting | bytes 6815744 | tf_op jit(solution)/shard_map/tile | solution.py:121
  72.8 102.4 %all-gather.6.cloned.1.call-done = bf16[160,56,832]{2,1,0:T(8,128)(2,1)} async-done(((bf16[5,56,832]{2,1,0:T(8,128)(2,1)}), bf16[160,56,832]{2,1,0:T(8,128)(2,1)}) %all-gather.6.cloned.1.call-update) | async-done | bytes 14909456 | tf_op jit(solution)/shard_map/all_gather | solution.py:87
  175.2 6.2 %slice_bitcast_fusion = (bf16[32,56,832]{2,1,0:T(8,128)(2,1)}, bf16[32,56,832]{2,1,0:T(8,128)(2,1)}) fusion(bf16[32,5,56,832]{3,2,1,0:T(8,128)(2,1)} %bitcast.78), kind=kLoop, calls=%fused_computation.25 | loop fusion | bytes 11927552 | tf_op jit(solution)/shard_map/reshape | solution.py:95
  181.4 9.5 %fusion.16 = bf16[3,512,832]{1,2,0:T(8,128)(2,1)S(1)} fusion(bf16[32,5,56,832]{3,2,1,0:T(8,128)(2,1)} %bitcast.79, bf16[512,32,52]{0,2,1:T(8,128)(2,1)S(1)} %copy-done.3), kind=kOutput, calls=%fused_computation.30 | convolution fusion | flops 4581457920 | bytes 19169280 | tf_op jit(solution)/shard_map/tgk,gckh->cth/dot_general | solution.py:103
  192.0 7.7 %fusion.51 = (f32[8,512]{1,0:T(8,128)S(1)}, f32[8,512,512]{1,2,0:T(8,128)}) fusion(pred[512,512]{0,1:T(8,128)(4,1)} %broadcast_compare_fusion, bf16[512,8,104]{0,2,1:T(8,128)(2,1)} %bitcast.85, bf16[512,8,104]{0,2,1:T(8,128)(2,1)S(1)} %bitcast.84), kind=kOutput, calls=%fused_computation.86 | convolution fusion | flops 444596736 | bytes 10371072 | tf_op jit(solution)/shard_map/sub | solution.py:26
  199.7 4.3 %fusion.19 = bf16[8,104,512]{2,1,0:T(8,128)(2,1)S(1)} fusion(bf16[512,8,104]{0,2,1:T(8,128)(2,1)S(1)} %bitcast.83, f32[8,512,512]{1,2,0:T(8,128)} %get-tuple-element.24, f32[8,512]{1,0:T(8,128)S(1)} %get-tuple-element.23), kind=kOutput, calls=%fused_computation.33 | convolution fusion | flops 440827904 | bytes 10108928 | tf_op jit(solution)/shard_map/hqk,khe->qhe/dot_general | solution.py:28
  204.0 3.9 %fusion.13 = f32[512,32,52]{0,2,1:T(8,128)} fusion(bf16[512,832,1]{0,1,2:T(8,128)(2,1)S(1)} %bitcast.96, bf16[32,56,832]{2,1,0:T(8,128)(2,1)S(1)} %copy-done.2), kind=kOutput, calls=%fused_computation.26 | convolution fusion | flops 1417674752 | bytes 7241728 | tf_op jit(solution)/shard_map/tf,gkf->tgk/dot_general | solution.py:111
  207.9 4.6 %reshape.133 = f32[512,1664]{0,1:T(8,128)} reshape(f32[512,32,52]{0,2,1:T(8,128)} %fusion.13) | data formatting | bytes 6815744 | tf_op jit(solution)/shard_map/reshape | solution.py:114
  212.6 2.4 fusion.20
  215.4 2.6 multiply_reduce_fusion
  218.4 4.0 %select_convert_fusion = bf16[512,1664]{0,1:T(8,128)(2,1)S(1)} fusion(f32[512,1664]{0,1:T(8,128)} %copy.51, f32[512]{0:T(512)S(1)} %mul.70, f32[512]{0:T(512)S(1)} %sub.34, pred[512]{0:T(512)(128)(4,1)S(1)} %broadcast_in_dim.52, f32[512,1664]{0,1:T(8,128)} %reshape.133, bf16[512,1664]{0,1:T(8,128)(2,1)S(1)} %copy.47), kind=kLoop, calls=%fused_computation.23 | loop fusion | flops 5963776 | bytes 10228224 | tf_op jit(solution)/shard_map/convert_element_type | solution.py:123
  222.4 1.4 copy.52
  223.8 2.1 reshape.136
  226.0 3.1 slice.93
  229.0 2.4 reshape.137
  231.4 3.4 pad_maximum_fusion
  234.9 6.3 %reshape.139 = bf16[32,59904]{1,0:T(8,128)(2,1)} reshape(bf16[32,72,832]{2,1,0:T(8,128)(2,1)} %pad_maximum_fusion) | data formatting | bytes 7667712 | tf_op jit(solution)/shard_map/reshape | solution.py:99
  241.2 2.0 slice-done
  243.2 3.0 reshape.140
  246.4 76.1 %collective-permute-done = bf16[6656,256]{1,0:T(8,128)(2,1)} collective-permute-done((bf16[6656,256]{1,0:T(8,128)(2,1)}, bf16[6656,256]{1,0:T(8,128)(2,1)}, u32[]{:S(2)}, u32[]{:S(2)}) %collective-permute-start) | collective-permute-done | bytes 3407904 | tf_op jit(solution)/shard_map/ppermute | solution.py:127
  322.4 6.0 %convolution_convert_fusion = bf16[512,256]{1,0:T(8,128)(2,1)S(1)} fusion(bf16[512,6656]{1,0:T(8,128)(2,1)} %all-gather.4.cloned.1.call-done, bf16[6656,256]{1,0:T(8,128)(2,1)} %collective-permute-done), kind=kOutput, calls=%fused_computation.35 | convolution fusion | flops 1744961536 | bytes 10485760 | tf_op jit(solution)/shard_map/dot_general | solution.py:128
  328.8 1.9 convolution_convert_fusion.1
  330.7 5.4 %collective-permute-done.1 = bf16[512,256]{1,0:T(8,128)(2,1)S(1)} collective-permute-done((bf16[512,256]{1,0:T(8,128)(2,1)S(1)}, bf16[512,256]{1,0:T(8,128)(2,1)S(1)}, u32[]{:S(2)}, u32[]{:S(2)}) %collective-permute-start.1) | collective-permute-done | bytes 262176 | tf_op jit(solution)/shard_map/ppermute | solution.py:129
  336.1 1.7 fusion.15
  337.7 36.3 %all_to_all.12 = bf16[32,64,256]{2,1,0:T(8,128)(2,1)S(1)} all-to-all(bf16[32,64,256]{2,1,0:T(8,128)(2,1)S(1)} %bitcast.82), channel_id=1, replica_groups=mesh['dp'=32,'yl'=2,'xx'=4] {'dp'}, dimensions={0} | all-to-all | bytes 2097152 | tf_op jit(solution)/shard_map/all_to_all | solution.py:140
  (73 shorter events, 12.6 us)
Async XLA Ops:
  6.5 33.9 %copy-start.6 = (f32[6656]{0:T(1024)S(1)}, f32[6656]{0:T(1024)}, u32[]{:S(2)}) copy-start(f32[6656]{0:T(1024)} %param.12) | copy-start | bytes 79876
  6.5 35.2 %copy-start.5 = (s32[1024,1]{0,1:T(1,128)S(1)}, s32[1024,1]{0,1:T(1,128)}, u32[]{:S(2)}) copy-start(s32[1024,1]{0,1:T(1,128)} %param.15) | copy-start | bytes 12292
  6.5 49.1 %copy-start.4 = (bf16[512,1664]{1,0:T(8,128)(2,1)S(1)}, bf16[512,1664]{1,0:T(8,128)(2,1)}, u32[]{:S(2)}) copy-start(bf16[512,1664]{1,0:T(8,128)(2,1)} %param.8) | copy-start | bytes 5111812
  6.5 168.7 %all-gather.6.cloned.1.call-start = ((), (), s32[]{:S(2)}) async-start(), calls=%async_computation.2 | async-start | bytes 16558080 | tf_op jit(solution)/shard_map/all_gather | solution.py:87
  40.4 282.0 %all-gather.4.cloned.1.call-start = ((), (), s32[]{:S(2)}) async-start(), calls=%async_computation.1 | async-start | bytes 8519680 | tf_op jit(solution)/shard_map/all_gather | solution.py:125
  55.6 2.2 copy-start.7
  175.2 6.2 %copy-start.3 = (bf16[512,32,52]{0,2,1:T(8,128)(2,1)S(1)}, bf16[512,32,52]{0,2,1:T(8,128)(2,1)}, u32[]{:S(2)}) copy-start(bf16[512,32,52]{0,2,1:T(8,128)(2,1)} %reshape.131) | copy-start | bytes 5111812
  199.7 4.3 %copy-start.2 = (bf16[32,56,832]{2,1,0:T(8,128)(2,1)S(1)}, bf16[32,56,832]{2,1,0:T(8,128)(2,1)}, u32[]{:S(2)}) copy-start(bf16[32,56,832]{2,1,0:T(8,128)(2,1)} %get-tuple-element.16) | copy-start | bytes 8945668
  225.9 5.5 %copy-start = (bf16[32,56,832]{2,1,0:T(8,128)(2,1)S(1)}, bf16[32,56,832]{2,1,0:T(8,128)(2,1)}, u32[]{:S(2)}) copy-start(bf16[32,56,832]{2,1,0:T(8,128)(2,1)} %get-tuple-element.15) | copy-start | bytes 8945668
  241.2 2.0 slice-start
  246.3 76.2 %collective-permute-start = (bf16[6656,256]{1,0:T(8,128)(2,1)}, bf16[6656,256]{1,0:T(8,128)(2,1)}, u32[]{:S(2)}, u32[]{:S(2)}) collective-permute-start(bf16[6656,256]{1,0:T(8,128)(2,1)} %reshape.140), channel_id=1, source_target_pairs={{0,4},{4,0},{1,5},{5,1},{2,6},{6,2},{3,7},{7,3},{8,12},{12,8},{9,1... | collective-permute-start | bytes 10223624 | tf_op jit(solution)/shard_map/ppermute | solution.py:127
  246.4 82.4 %copy-start.1 = (bf16[6656,256]{1,0:T(8,128)(2,1)S(1)}, bf16[6656,256]{1,0:T(8,128)(2,1)}, u32[]{:S(2)}) copy-start(bf16[6656,256]{1,0:T(8,128)(2,1)} %reshape.140) | copy-start | bytes 10223620
  322.4 6.4 %copy-start.8 = (bf16[512,6656]{1,0:T(8,128)(2,1)S(1)}, bf16[512,6656]{1,0:T(8,128)(2,1)}, u32[]{:S(2)}) copy-start(bf16[512,6656]{1,0:T(8,128)(2,1)} %all-gather.4.cloned.1.call-done) | copy-start | bytes 20447236
  328.4 7.7 %collective-permute-start.1 = (bf16[512,256]{1,0:T(8,128)(2,1)S(1)}, bf16[512,256]{1,0:T(8,128)(2,1)S(1)}, u32[]{:S(2)}, u32[]{:S(2)}) collective-permute-start(bf16[512,256]{1,0:T(8,128)(2,1)S(1)} %convolution_convert_fusion), channel_id=1, source_target_pairs={{0,4},{4,0},{1,5},{5,1},{2,6},{6,2},{3,7},{7,3},{8,12},{12,8},{9,1... | collective-permute-start | bytes 786440 | tf_op jit(solution)/shard_map/ppermute | solution.py:129
Sparse Core Ops, SparseCore 0:
  40.5 134.6 all-gather.5
  226.1 69.6 all-gather.3

commit v10 on v8

--- a/solution.py
+++ b/solution.py
@@ -125,15 +125,16 @@
     theirs = jnp.dot(rows_x, merge_full[:, cols:], preferred_element_type=jnp.float32)
     swapped = lax.ppermute(theirs.astype(jnp.bfloat16), "yl", [(0, 1), (1, 0)])
     own = jnp.dot(rows_x, merge_full[:, :cols], preferred_element_type=jnp.float32)
-    own, swapped = lax.optimization_barrier((own.astype(jnp.bfloat16), swapped))
-    features = jnp.where(
-        y_low == 0,
-        jnp.concatenate([own, swapped], axis=0),
-        jnp.concatenate([swapped, own], axis=0),
-    )
-    group_rows = features.shape[0]
+    own = own.astype(jnp.bfloat16)
+    half = own.shape[0]
+    group_rows = 2 * half
     pick = (source_row[:, None] == jnp.arange(group_rows, dtype=jnp.int32)[None, :]).astype(jnp.bfloat16)
-    outgoing = jnp.dot(pick, features, preferred_element_type=jnp.float32).astype(jnp.bfloat16)
+    first = y_low == 0
+    pick_own = jnp.where(first, pick[:, :half], pick[:, half:])
+    pick_swap = jnp.where(first, pick[:, half:], pick[:, :half])
+    part = jnp.dot(pick_own, own, preferred_element_type=jnp.float32)
+    outgoing = part + jnp.dot(pick_swap, swapped, preferred_element_type=jnp.float32)
+    outgoing = outgoing.astype(jnp.bfloat16)
     return lax.all_to_all(outgoing, "dp", split_axis=0, concat_axis=0, tiled=True)
 
 

time: 376 us -> 379 us (level)
  matrix products: 35 us -> 42.9 us
  waiting for transfers between devices: 172 us -> 165 us
    dot_general x2, matrix products: 3.6 us -> 11.7 us  [the longest x1 8.76 us: local(): part = jnp.dot(pick_own, own, preferred_element_type=jnp.float32)]
    ppermute x1, waiting for transfers between devices: 4.5 us -> 0.01 us  [local(): swapped = lax.ppermute(theirs.astype(jnp.bfloat16), 'yl', [(0, 1), (1, 0)])]
  transfers between devices with their start and end apart: 4 -> 4, of which waited for: 3 -> 2; matrix products, arithmetic and copies ran while one was open for 16% -> 18% of each run, Pallas kernels for 0% -> 0%
where the time goes in v10:
time: 379 us; the launch traced here: 376 us
  waiting for transfers between devices  165 us (44%)
  blocking collectives  67.5 us (18%)
  local copies, waits for them, and re-layouts  55.8 us (15%)
  matrix products  42.9 us (11%)
  other arithmetic  28.9 us (8%)
  between operations  13.7 us (4%)
    all_gather x1, waiting for transfers between devices, local(): gathered = lax.all_gather(payload, 'dp', axis=0, tiled=False)  123 us
    all_gather x1, waiting for transfers between devices, local(): rows_x = lax.all_gather(merged, 'xx', axis=0, tiled=True)  41.5 us
    all_to_all x1, blocking collectives, local(): lax.all_to_all(outgoing, 'dp', split_axis=0, concat_axis=0, tiled=True)  38.8 us
    all_gather x1, blocking collectives, local(): lax.all_gather(jnp.concatenate(slabs, axis=0), ('yl', 'xx'), axis=1, tile...  28.7 us
    another operation x1, local copies, waits for them, and re-layouts, local(): merge_full.reshape(n_dp, -1)[:, :both.size].reshape(-1, both.shape[1])  15.4 us
    dot_general x1, matrix products, local(): jnp.einsum('tgk,gckh->cth', normed, weights[:, :3], preferred_element_typ...  9.35 us
    another operation x3, other arithmetic  9.15 us
    dot_general x1, matrix products, local(): part = jnp.dot(pick_own, own, preferred_element_type=jnp.float32)  8.76 us
  transfers between devices with their start and end apart: 4, of which 2 were waited for; matrix products, arithmetic and copies ran while one was open for 18% of the time, Pallas kernels for 0%

profile of v10, /device:TPU:30, one launch (start us, length us, event | category | flops | bytes accessed | tf_op | source)
XLA Modules:
  0.0 375.8 jit_solution(1339185545670524082)
XLA Ops:
  9.3 28.7 %all_gather.12 = bf16[224,832]{0,1:T(8,128)(2,1)S(1)} all-gather(bf16[224,104]{0,1:T(8,128)(2,1)S(1)} %fusion.55), channel_id=1, replica_groups=mesh['dp'=32,'yl'=2,'xx'=4] {'yl','xx'}, dimensions={1}, use_global_device_ids=true | all-gather | bytes 419328 | tf_op jit(solution)/shard_map/all_gather | solution.py:71
  42.2 2.4 tile.12
  44.7 4.9 %copy.56 = f32[512,1664]{0,1:T(8,128)} copy(f32[512,1664]{1,0:T(8,128)} %tile.12) | data formatting | bytes 6815744 | tf_op jit(solution)/shard_map/tile | solution.py:119
  50.5 9.0 %reduce-window.6 = s32[32,8,128]{2,1,0:T(8,128)S(1)} reduce-window(s32[32,8,128]{2,1,0:T(8,128)S(1)} %fusion.46, s32[]{:T(128)} %constant.20.clone.1), window={size=1x1x128 pad=0_0x0_0x127_0}, to_apply=%region_0.1 | reduce-window | flops 4161536 | bytes 262148 | tf_op jit(solution)/shard_map/reduce-window
  60.0 4.5 %scatter_custom_fusion = s32[2048]{0:T(1024)S(1)} fusion(s32[1024]{0:T(1024)S(1)} %bitcast.94, s32[1024]{0:T(1024)S(1)} %iota.15, s32[]{:T(128)} %constant.11.clone.1), kind=kCustom, calls=%fused_computation.80 | custom fusion | bytes 8196 | tf_op jit(solution)/shard_map/scatter | solution.py:55
  64.5 1.4 copy.52
  67.3 1.4 reshape.126
  68.7 123.4 %all-gather.6.cloned.1.call-done = bf16[192,56,832]{2,1,0:T(8,128)(2,1)} async-done(((bf16[6,56,832]{2,1,0:T(8,128)(2,1)}), bf16[192,56,832]{2,1,0:T(8,128)(2,1)}) %all-gather.6.cloned.1.call-update) | async-done | bytes 17891344 | tf_op jit(solution)/shard_map/all_gather | solution.py:88
  192.1 3.8 %slice_bitcast_fusion = bf16[32,56,832]{2,1,0:T(8,128)(2,1)} fusion(bf16[32,6,56,832]{3,2,1,0:T(8,128)(2,1)} %bitcast.74), kind=kLoop, calls=%fused_computation.30 | loop fusion | bytes 5963776 | tf_op jit(solution)/shard_map/squeeze | solution.py:110
  195.9 9.3 %fusion.19 = bf16[3,512,832]{1,2,0:T(8,128)(2,1)S(1)} fusion(bf16[32,6,56,832]{3,2,1,0:T(8,128)(2,1)} %bitcast.75, bf16[512,32,52]{0,2,1:T(8,128)(2,1)S(1)} %copy-done.1), kind=kOutput, calls=%fused_computation.33 | convolution fusion | flops 4581457920 | bytes 22151168 | tf_op jit(solution)/shard_map/tgk,gckh->cth/dot_general | solution.py:101
  205.3 1.1 fusion.62
  206.4 7.8 %fusion.64 = (f32[8,512]{1,0:T(8,128)S(1)}, f32[8,512,512]{1,2,0:T(8,128)}) fusion(pred[512,512]{0,1:T(8,128)(4,1)} %broadcast_compare_fusion, bf16[512,8,104]{0,2,1:T(8,128)(2,1)} %bitcast.84, bf16[512,8,104]{0,2,1:T(8,128)(2,1)S(1)} %bitcast.83), kind=kOutput, calls=%fused_computation.91 | convolution fusion | flops 444596736 | bytes 10371072 | tf_op jit(solution)/shard_map/sub | solution.py:26
  214.2 4.3 %fusion.31 = bf16[8,104,512]{2,1,0:T(8,128)(2,1)S(1)} fusion(bf16[512,8,104]{0,2,1:T(8,128)(2,1)S(1)} %bitcast.82, f32[8,512,512]{1,2,0:T(8,128)} %get-tuple-element.18, f32[8,512]{1,0:T(8,128)S(1)} %get-tuple-element.17), kind=kOutput, calls=%fused_computation.45 | convolution fusion | flops 440827904 | bytes 10108928 | tf_op jit(solution)/shard_map/hqk,khe->qhe/dot_general | solution.py:28
  218.5 3.9 %fusion.16 = f32[512,32,52]{0,2,1:T(8,128)} fusion(bf16[512,832,1]{0,1,2:T(8,128)(2,1)S(1)} %bitcast.95, bf16[32,56,832]{2,1,0:T(8,128)(2,1)S(1)} %copy-done), kind=kOutput, calls=%fused_computation.28 | convolution fusion | flops 1417674752 | bytes 7241728 | tf_op jit(solution)/shard_map/tf,gkf->tgk/dot_general | solution.py:109
  222.5 4.7 %reshape.128 = f32[512,1664]{0,1:T(8,128)} reshape(f32[512,32,52]{0,2,1:T(8,128)} %fusion.16) | data formatting | bytes 6815744 | tf_op jit(solution)/shard_map/reshape | solution.py:112
  227.2 2.4 fusion.32
  230.0 2.6 multiply_reduce_fusion
  233.0 4.0 %select_convert_fusion = bf16[512,1664]{0,1:T(8,128)(2,1)S(1)} fusion(f32[512,1664]{0,1:T(8,128)} %copy.56, f32[512]{0:T(512)S(1)} %mul.70, f32[512]{0:T(512)S(1)} %sub.34, pred[512]{0:T(512)(128)(4,1)S(1)} %broadcast_in_dim.52, f32[512,1664]{0,1:T(8,128)} %reshape.128, bf16[512,1664]{0,1:T(8,128)(2,1)S(1)} %copy.52), kind=kLoop, calls=%fused_computation.26 | loop fusion | flops 5963776 | bytes 10228224 | tf_op jit(solution)/shard_map/convert_element_type | solution.py:121
  237.1 1.4 copy.57
  238.5 2.1 reshape.131
  240.6 2.5 fusion.1
  243.1 3.3 slice.109
  246.4 2.0 slice.108
  248.9 4.6 %pad_maximum_fusion = bf16[32,128,832]{2,1,0:T(8,128)(2,1)} fusion(bf16[32,112,832]{2,1,0:T(8,128)(2,1)S(1)} %bitcast.73, bf16[32,16,832]{2,1,0:T(8,128)(2,1)S(1)} %copy.59), kind=kLoop, calls=%fused_computation.7 | loop fusion | flops 13631488 | bytes 13631488 | tf_op jit(solution)/shard_map/concatenate | solution.py:93
  253.5 15.4 %reshape_reshape.3 = bf16[6656,512]{1,0:T(8,128)(2,1)} reshape(bf16[32,128,832]{2,1,0:T(8,128)(2,1)} %pad_maximum_fusion) | data formatting | bytes 13631488 | tf_op jit(solution)/shard_map/reshape;reshape | solution.py:97
  268.9 41.5 %all-gather.4.cloned.1.call-done = bf16[512,6656]{1,0:T(8,128)(2,1)} async-done(((bf16[128,6656]{1,0:T(8,128)(2,1)}), bf16[512,6656]{1,0:T(8,128)(2,1)}) %all-gather.4.cloned.1.call-update) | async-done | bytes 6815760 | tf_op jit(solution)/shard_map/all_gather | solution.py:123
  310.4 5.8 %fusion.36 = bf16[512,256]{1,0:T(8,128)(2,1)S(1)} fusion(bf16[512,6656]{1,0:T(8,128)(2,1)} %all-gather.4.cloned.1.call-done, bf16[6656,512]{1,0:T(8,128)(2,1)} %reshape_reshape.3), kind=kOutput, calls=%fused_computation.48 | convolution fusion | flops 1744961536 | bytes 10485760 | tf_op jit(solution)/shard_map/dot_general | solution.py:125
  316.2 1.2 collective-permute-start.1
  317.4 8.8 %fusion.21 = f32[2048,256]{1,0:T(8,128)S(1)} fusion(pred[]{:T(512)S(6)} %eq.58, bf16[2048,1024]{1,0:T(8,128)(2,1)} %fusion.1, bf16[512,6656]{1,0:T(8,128)(2,1)} %all-gather.4.cloned.1.call-done, bf16[6656,512]{1,0:T(8,128)(2,1)} %reshape_reshape.3), kind=kOutput, calls=%fused_computation.35 | convolution fusion | flops 2282881024 | bytes 16515073 | tf_op jit(solution)/shard_map/dot_general | solution.py:135
  326.2 3.0 fusion.18
  329.1 38.8 %all_to_all.12 = bf16[32,64,256]{2,1,0:T(8,128)(2,1)S(1)} all-to-all(bf16[32,64,256]{2,1,0:T(8,128)(2,1)S(1)} %bitcast.81), channel_id=1, replica_groups=mesh['dp'=32,'yl'=2,'xx'=4] {'dp'}, dimensions={0} | all-to-all | bytes 2097152 | tf_op jit(solution)/shard_map/all_to_all | solution.py:138
  368.0 1.0 copy.71
  (68 shorter events, 11.0 us)
Async XLA Ops:
  6.5 35.2 %copy-start.4 = (f32[6656]{0:T(1024)S(1)}, f32[6656]{0:T(1024)}, u32[]{:S(2)}) copy-start(f32[6656]{0:T(1024)} %param.12) | copy-start | bytes 79876
  6.5 185.6 %all-gather.6.cloned.1.call-start = ((), (), s32[]{:S(2)}) async-start(), calls=%async_computation.2 | async-start | bytes 19869696 | tf_op jit(solution)/shard_map/all_gather | solution.py:88
  6.5 32.6 %collective-permute-start = (bf16[208,256]{1,0:T(8,128)(2,1)}, bf16[208,256]{1,0:T(8,128)(2,1)S(1)}, u32[]{:S(2)}, u32[]{:S(2)}) collective-permute-start(bf16[208,256]{1,0:T(8,128)(2,1)} %param.13), channel_id=1, source_target_pairs={{0,4},{4,0},{1,5},{5,1},{2,6},{6,2},{3,7},{7,3},{8,12},{12,8},{9,1... | collective-permute-start | bytes 319496 | tf_op jit(solution)/shard_map/ppermute | solution.py:70
  40.5 269.9 %all-gather.4.cloned.1.call-start = ((), (), s32[]{:S(2)}) async-start(), calls=%async_computation.1 | async-start | bytes 8519680 | tf_op jit(solution)/shard_map/all_gather | solution.py:123
  44.6 5.8 %copy-start.3 = (s32[1024,1]{0,1:T(1,128)S(1)}, s32[1024,1]{0,1:T(1,128)}, u32[]{:S(2)}) copy-start(s32[1024,1]{0,1:T(1,128)} %param.15) | copy-start | bytes 12292
  44.7 19.9 %copy-start.2 = (bf16[512,1664]{1,0:T(8,128)(2,1)S(1)}, bf16[512,1664]{1,0:T(8,128)(2,1)}, u32[]{:S(2)}) copy-start(bf16[512,1664]{1,0:T(8,128)(2,1)} %param.8) | copy-start | bytes 5111812
  64.5 2.2 copy-start.5
  68.7 127.2 %copy-start.1 = (bf16[512,32,52]{0,2,1:T(8,128)(2,1)S(1)}, bf16[512,32,52]{0,2,1:T(8,128)(2,1)}, u32[]{:S(2)}) copy-start(bf16[512,32,52]{0,2,1:T(8,128)(2,1)} %reshape.126) | copy-start | bytes 5111812
  214.2 4.3 %copy-start = (bf16[32,56,832]{2,1,0:T(8,128)(2,1)S(1)}, bf16[32,56,832]{2,1,0:T(8,128)(2,1)}, u32[]{:S(2)}) copy-start(bf16[32,56,832]{2,1,0:T(8,128)(2,1)} %slice_bitcast_fusion) | copy-start | bytes 8945668
  316.2 10.0 %collective-permute-start.1 = (bf16[512,256]{1,0:T(8,128)(2,1)S(1)}, bf16[512,256]{1,0:T(8,128)(2,1)S(1)}, u32[]{:S(2)}, u32[]{:S(2)}) collective-permute-start(bf16[512,256]{1,0:T(8,128)(2,1)S(1)} %fusion.36), channel_id=1, source_target_pairs={{0,4},{4,0},{1,5},{5,1},{2,6},{6,2},{3,7},{7,3},{8,12},{12,8},{9,1... | collective-permute-start | bytes 786440 | tf_op jit(solution)/shard_map/ppermute | solution.py:126
Sparse Core Ops, SparseCore 0:
  40.6 151.4 all-gather.5
  240.7 69.6 all-gather.3
